TPU v7x, 32 devices: a whole 2x2x4 slice. The times are simulated.
32 devices in a mesh: outer: 4 (over z), inner: 8 (over y, x, core).
Axes of the slice: x: 2, y: 2, z: 4, core: 2. Of those that a mesh axis runs over, the one named last changes fastest.
Arguments:
- queries: bfloat16 [8192, 1024], P(('outer', 'inner')), may hold values from -60 to 60
- key_states: bfloat16 [8192, 128], P(('outer', 'inner')), may hold values from -6 to 6
- value_states: bfloat16 [8192, 128], P(('outer', 'inner')), may hold values from -6 to 6
- grad_output: bfloat16 [8192, 1024], P(('outer', 'inner')), may hold values from -6 to 6
- documents: int32 [8192], replicated, may hold values from 0 to 20, never falling along the last dimension, each value on 1 to 768 neighbouring positions
- block_order: int32 [64], replicated, may hold values from 0 to 63, as said below
Outputs:
- grad_queries: bfloat16 [8192, 1024], P(('outer', 'inner'))
- grad_keys: bfloat16 [8192, 128], P(('outer', 'inner'))
- grad_values: bfloat16 [8192, 128], P(('outer', 'inner'))
Inputs may be any that keep to these rules, and one draw needn't show every extreme that they name: `documents`: never falling along the sequence; every document has 1 to 768 positions and one has exactly 768. `block_order`: device d of the joined index outer, inner (d = outer * 8 + inner) holds stored blocks 2 * d and 2 * d + 1, which are sequence blocks d and 63 - d in either order.
All inputs are finite; a program needn't handle non-finite values.
Results may differ from a plain program's by a relative error of at most 0.0049.
Values may be sent and summed in bfloat16 or wider, within the bound.
No kernel may reach another device: no remote copies, remote signals or barrier semaphores. Data moves between devices by JAX's collectives and lax.ppermute only.
A program may use at most 64 MiB of HBM per device.

v0:
```python
import math

import jax
import jax.numpy as jnp
from jax import lax
from jax.sharding import PartitionSpec as P


REACH = 6

NEGATIVE = -1e30

AXES = ("outer", "inner")


def fold_source(r, j):
    if j <= r:
        return ("high", j)
    gap = 2 * r + 1 - j
    if gap > 0:
        return ("above", gap)
    if gap == 0:
        return ("own", 0)
    return ("below", -gap)


def on_device(queries, key_states, value_states, grad_output, documents, block_order):
    count = lax.axis_size(AXES)
    device = lax.axis_index(AXES)
    length = key_states.shape[0] // 2
    head_size = key_states.shape[1]
    factor = 1.0 / math.sqrt(head_size)
    span = REACH + 1

    first_slot = jnp.where(block_order[2 * device] < count, 0, 1).astype(jnp.int32)
    second_slot = 1 - first_slot

    def take_block(rows, slot):
        return lax.dynamic_slice_in_dim(rows, slot * length, length, 0)

    joined = jnp.concatenate([key_states, value_states], 1)
    low = take_block(joined, first_slot)
    high = take_block(joined, second_slot)
    odd = (device % 2) == 1
    own = jnp.stack([low, high])
    mate = lax.ppermute(own, AXES, [(s, s ^ 1) for s in range(count)])
    even_part = jnp.where(odd, mate, own)
    odd_part = jnp.where(odd, own, mate)
    chip = jnp.stack([even_part[0], odd_part[0], even_part[1], odd_part[1]])
    lows = {0: chip[0], 1: chip[1]}
    highs = {0: chip[2], 1: chip[3]}
    for j in range(1, REACH // 2 + 1):
        up = [(s, s + 2 * j) for s in range(count - 2 * j)]
        down = [(s, s - 2 * j) for s in range(2 * j, count)]
        below_chip = lax.ppermute(chip[:2], AXES, up)
        above_chip = lax.ppermute(chip, AXES, down)
        lows[-2 * j], lows[1 - 2 * j] = below_chip[0], below_chip[1]
        lows[2 * j], lows[2 * j + 1] = above_chip[0], above_chip[1]
        highs[2 * j], highs[2 * j + 1] = above_chip[2], above_chip[3]

    def by_parity(table, t):
        return jnp.where(odd, table[t + 1], table[t])

    low_window = jnp.concatenate([by_parity(lows, t) for t in range(-REACH, 1)], 0)

    fold_index = jnp.clip(count - 1 - device, 0, REACH)

    def fold_block(r, j):
        parity = (count - 1 - r) % 2
        kind, at = fold_source(r, j)
        return lows[parity + {"above": at, "own": 0, "below": -at}[kind]]

    pieces = []
    for j in range(REACH, 0, -1):
        block = by_parity(highs, j)
        for r in range(j - 1, -1, -1):
            block = jnp.where(fold_index == r, fold_block(r, j), block)
        pieces.append(block)
    high_window = jnp.concatenate(pieces + [by_parity(highs, 0)], 0)
    windows = jnp.stack([low_window, high_window])
    key_window = windows[..., :head_size]
    value_window = windows[..., head_size:]

    def split_heads(rows):
        return rows.reshape(rows.shape[0], rows.shape[1] // head_size, head_size)

    query_pair = jnp.stack(
        [split_heads(take_block(queries, first_slot)), split_heads(take_block(queries, second_slot))]
    )
    output_pair = jnp.stack(
        [
            split_heads(take_block(grad_output, first_slot)),
            split_heads(take_block(grad_output, second_slot)),
        ]
    )

    pad = REACH * length
    padded_documents = jnp.concatenate([jnp.full((pad,), -1, documents.dtype), documents])
    query_blocks = (device, 2 * count - 1 - device)
    offsets = jnp.arange(length, dtype=jnp.int32)
    window_offsets = jnp.arange(span * length, dtype=jnp.int32)
    query_place = jnp.stack([b * length + offsets for b in query_blocks])
    key_place = jnp.stack([b * length - pad + window_offsets for b in query_blocks])
    query_owner = jnp.stack(
        [lax.dynamic_slice_in_dim(documents, b * length, length) for b in query_blocks]
    )
    key_owner = jnp.stack(
        [lax.dynamic_slice_in_dim(padded_documents, b * length, span * length) for b in query_blocks]
    )
    allowed = (
        (key_place[:, None, :] >= 0)
        & (key_place[:, None, :] <= query_place[:, :, None])
        & (key_owner[:, None, :] == query_owner[:, :, None])
    )[:, None]

    scores = (
        jnp.einsum("qbhd,qwd->qhbw", query_pair, key_window, preferred_element_type=jnp.float32)
        * factor
    )
    grad_prob = jnp.einsum(
        "qbhd,qwd->qhbw", output_pair, value_window, preferred_element_type=jnp.float32
    )
    masked = jnp.where(allowed, scores, NEGATIVE)
    top = masked.max(-1)
    weights = jnp.where(allowed, jnp.exp(scores - top[..., None]), 0.0)
    log_totals = top + jnp.log(weights.sum(-1))
    probabilities = jnp.where(allowed, jnp.exp(scores - log_totals[..., None]), 0.0)
    row_dots = (probabilities * grad_prob).sum(-1)
    grad_scores = probabilities * (grad_prob - row_dots[..., None])
    rounded_probs = probabilities.astype(jnp.bfloat16)
    rounded_grads = grad_scores.astype(jnp.bfloat16)

    grad_query = jnp.einsum(
        "qhbw,qwd->qbhd", rounded_grads, key_window, preferred_element_type=jnp.float32
    )
    grad_key = jnp.einsum(
        "qhbw,qbhd->qwd", rounded_grads, query_pair, preferred_element_type=jnp.float32
    )
    grad_value = jnp.einsum(
        "qhbw,qbhd->qwd", rounded_probs, output_pair, preferred_element_type=jnp.float32
    )
    parts = jnp.concatenate([grad_key, grad_value], -1).reshape(2, span, length, 2 * head_size)
    low_parts = parts[0]
    high_parts = parts[1]

    zero = jnp.zeros_like(high_parts[0])
    routed = {}
    for r in range(REACH):
        for j in range(r + 1, REACH + 1):
            routed.setdefault(fold_source(r, j), []).append((r, j))

    def routed_to(kind, at):
        block = zero
        for r, j in routed.get((kind, at), []):
            block = jnp.where(fold_index == r, high_parts[REACH - j], block)
        return block

    to_high = [jnp.where(fold_index >= j, high_parts[REACH - j], zero) for j in range(1, REACH + 1)]
    to_above_low = [routed_to("above", m) for m in range(1, REACH + 1)]
    to_below = [routed_to("below", m) for m in range(1, REACH + 1)]
    to_own_low = routed_to("own", 0)

    grad_low = low_parts[REACH] + to_own_low
    grad_high = high_parts[REACH]
    for k in range(1, REACH + 1):
        up = [(s + k, s) for s in range(count - k)]
        down = [(s - k, s) for s in range(k, count)]
        sent_low = lax.ppermute(low_parts[REACH - k] + to_below[k - 1], AXES, up)
        back = lax.ppermute(jnp.concatenate([to_above_low[k - 1], to_high[k - 1]], 0), AXES, down)
        grad_low = grad_low + sent_low
        grad_low = grad_low + back[:length]
        grad_high = grad_high + back[length:]

    grad_query = (
        (grad_query * factor)
        .astype(jnp.bfloat16)
        .reshape(2, length, query_pair.shape[2] * head_size)
    )
    grad_kv = jnp.stack([grad_low, grad_high])
    grad_keys = (grad_kv[:, :, :head_size] * factor).astype(jnp.bfloat16)
    grad_values = grad_kv[:, :, head_size:].astype(jnp.bfloat16)

    def restore(paired):
        return jnp.concatenate([paired[first_slot], paired[second_slot]], 0)

    return (restore(grad_query), restore(grad_keys), restore(grad_values))


def solution(mesh):
    in_specs = (
        P(AXES, None),
        P(AXES, None),
        P(AXES, None),
        P(AXES, None),
        P(),
        P(),
    )
    out_specs = (
        P(AXES, None),
        P(AXES, None),
        P(AXES, None),
    )

    return jax.shard_map(on_device, mesh=mesh, in_specs=in_specs, out_specs=out_specs, check_vma=False)
```

profile of v0, /device:TPU:21, one launch (start us, length us, event | category | flops | bytes accessed | tf_op | source)
XLA Modules:
  0.0 112.3 jit_solution(17665163538900593014)
XLA Ops:
  8.3 4.1 %collective-permute-start.1 = (bf16[2,128,256]{2,1,0:T(8,128)(2,1)S(1)}, bf16[2,128,256]{2,1,0:T(8,128)(2,1)S(1)}, u32[]{:S(2)}, u32[]{:S(2)}) collective-permute-start(bf16[2,128,256]{2,1,0:T(8,128)(2,1)S(1)} %pad_maximum_fusion.17), channel_id=1, source_target_pairs={{0,6},{1,7},{2,8},{3,9},{4,10},{5,11},{6,12},{7,13},{8,14},{9,15},... | collective-permute-start | bytes 393224 | tf_op jit(solution)/shard_map/ppermute | solution.py:55
  15.2 2.1 %collective-permute-start.4 = (bf16[4,128,256]{2,1,0:T(8,128)(2,1)S(1)}, bf16[4,128,256]{2,1,0:T(8,128)(2,1)S(1)}, u32[]{:S(2)}, u32[]{:S(2)}) collective-permute-start(bf16[4,128,256]{2,1,0:T(8,128)(2,1)S(1)} %pad_maximum_fusion.8), channel_id=1, source_target_pairs={{4,0},{5,1},{6,2},{7,3},{8,4},{9,5},{10,6},{11,7},{12,8},{13,9},{1... | collective-permute-start | bytes 786440 | tf_op jit(solution)/shard_map/ppermute | solution.py:56
  17.4 2.0 %collective-permute-start.5 = (bf16[4,128,256]{2,1,0:T(8,128)(2,1)S(1)}, bf16[4,128,256]{2,1,0:T(8,128)(2,1)S(1)}, u32[]{:S(2)}, u32[]{:S(2)}) collective-permute-start(bf16[4,128,256]{2,1,0:T(8,128)(2,1)S(1)} %pad_maximum_fusion.8), channel_id=1, source_target_pairs={{6,0},{7,1},{8,2},{9,3},{10,4},{11,5},{12,6},{13,7},{14,8},{15,9},... | collective-permute-start | bytes 786440 | tf_op jit(solution)/shard_map/ppermute | solution.py:56
  19.4 4.0 %collective-permute-start.2 = (bf16[2,128,256]{2,1,0:T(8,128)(2,1)S(1)}, bf16[2,128,256]{2,1,0:T(8,128)(2,1)S(1)}, u32[]{:S(2)}, u32[]{:S(2)}) collective-permute-start(bf16[2,128,256]{2,1,0:T(8,128)(2,1)S(1)} %pad_maximum_fusion.17), channel_id=1, source_target_pairs={{0,4},{1,5},{2,6},{3,7},{4,8},{5,9},{6,10},{7,11},{8,12},{9,13},{1... | collective-permute-start | bytes 393224 | tf_op jit(solution)/shard_map/ppermute | solution.py:55
  23.5 3.1 %collective-permute-start.6 = (bf16[4,128,256]{2,1,0:T(8,128)(2,1)S(1)}, bf16[4,128,256]{2,1,0:T(8,128)(2,1)S(1)}, u32[]{:S(2)}, u32[]{:S(2)}) collective-permute-start(bf16[4,128,256]{2,1,0:T(8,128)(2,1)S(1)} %pad_maximum_fusion.8), channel_id=1, source_target_pairs={{2,0},{3,1},{4,2},{5,3},{6,4},{7,5},{8,6},{9,7},{10,8},{11,9},{12,... | collective-permute-start | bytes 786440 | tf_op jit(solution)/shard_map/ppermute | solution.py:56
  26.5 2.2 %collective-permute-start.3 = (bf16[2,128,256]{2,1,0:T(8,128)(2,1)S(1)}, bf16[2,128,256]{2,1,0:T(8,128)(2,1)S(1)}, u32[]{:S(2)}, u32[]{:S(2)}) collective-permute-start(bf16[2,128,256]{2,1,0:T(8,128)(2,1)S(1)} %pad_maximum_fusion.17), channel_id=1, source_target_pairs={{0,2},{1,3},{2,4},{3,5},{4,6},{5,7},{6,8},{7,9},{8,10},{9,11},{10,... | collective-permute-start | bytes 393224 | tf_op jit(solution)/shard_map/ppermute | solution.py:55
  28.8 5.9 %collective-permute-done.2 = bf16[2,128,256]{2,1,0:T(8,128)(2,1)S(1)} collective-permute-done((bf16[2,128,256]{2,1,0:T(8,128)(2,1)S(1)}, bf16[2,128,256]{2,1,0:T(8,128)(2,1)S(1)}, u32[]{:S(2)}, u32[]{:S(2)}) %collective-permute-start.2) | collective-permute-done | bytes 131104 | tf_op jit(solution)/shard_map/ppermute | solution.py:55
  34.8 5.5 %collective-permute-done.3 = bf16[2,128,256]{2,1,0:T(8,128)(2,1)S(1)} collective-permute-done((bf16[2,128,256]{2,1,0:T(8,128)(2,1)S(1)}, bf16[2,128,256]{2,1,0:T(8,128)(2,1)S(1)}, u32[]{:S(2)}, u32[]{:S(2)}) %collective-permute-start.3) | collective-permute-done | bytes 131104 | tf_op jit(solution)/shard_map/ppermute | solution.py:55
  43.4 2.0 %fusion = (f32[2,8,128]{2,1,0:T(8,128)S(1)}, f32[2,896,128,8]{2,1,3,0:T(8,128)S(1)}) fusion(f32[2,896,128,8]{2,1,3,0:T(8,128)S(1)} %get-tuple-element.61, f32[2,8,128]{2,1,0:T(8,128)S(1)} %log_add_fusion, pred[2,128,896]{1,2,0:T(8,128)(4,1)S(1)} %compare_and_fusion, bf16[1,128,8,128]{3,1,2,0:T(8,128)(2,1)S(1)} %copy.26, ...), kind=kOutput, calls=%fused_computation.2 | convolution fusion | flops 480901120 | bytes 16367616 | tf_op jit(solution)/shard_map/qbhd,qwd->qhbw/dot_general | solution.py:120
  46.8 2.1 %fusion.2 = bf16[2,8,128,896]{2,3,1,0:T(8,128)(2,1)S(1)} fusion(f32[2,896,128,8]{2,1,3,0:T(8,128)S(1)} %get-tuple-element.63, f32[2,896,128,8]{2,1,3,0:T(8,128)S(1)} %get-tuple-element.61, f32[2,8,128]{2,1,0:T(8,128)S(1)} %get-tuple-element.62, f32[2,8,128]{2,1,0:T(8,128)S(1)} %log_add_fusion, pred[2,128,896]{1,2,0:T(8,128)(4,1)S(1)} %compare_and_fusion), kind=kLoop, calls=%fused_computation.4 | loop fusion | flops 11010048 | bytes 18595840 | tf_op jit(solution)/shard_map/convert_element_type | solution.py:131
  51.6 1.9 %collective-permute-start.8 = (f32[256,256]{1,0:T(8,128)S(1)}, f32[256,256]{1,0:T(8,128)S(1)}, u32[]{:S(2)}, u32[]{:S(2)}) collective-permute-start(f32[256,256]{1,0:T(8,128)S(1)} %pad_maximum_fusion.9), channel_id=1, source_target_pairs={{0,1},{1,2},{2,3},{3,4},{4,5},{5,6},{6,7},{7,8},{8,9},{9,10},{10,1... | collective-permute-start | bytes 786440 | tf_op jit(solution)/shard_map/ppermute | solution.py:169
  54.4 1.9 %collective-permute-start.10 = (f32[256,256]{1,0:T(8,128)}, f32[256,256]{1,0:T(8,128)}, u32[]{:S(2)}, u32[]{:S(2)}) collective-permute-start(f32[256,256]{1,0:T(8,128)} %pad_maximum_fusion.10), channel_id=1, source_target_pairs={{0,2},{1,3},{2,4},{3,5},{4,6},{5,7},{6,8},{7,9},{8,10},{9,11},{10,... | collective-permute-start | bytes 786440 | tf_op jit(solution)/shard_map/ppermute | solution.py:169
  56.3 1.9 %collective-permute-start.12 = (f32[256,256]{1,0:T(8,128)S(1)}, f32[256,256]{1,0:T(8,128)}, u32[]{:S(2)}, u32[]{:S(2)}) collective-permute-start(f32[256,256]{1,0:T(8,128)S(1)} %pad_maximum_fusion.11), channel_id=1, source_target_pairs={{0,3},{1,4},{2,5},{3,6},{4,7},{5,8},{6,9},{7,10},{8,11},{9,12},{10... | collective-permute-start | bytes 786440 | tf_op jit(solution)/shard_map/ppermute | solution.py:169
  58.3 4.9 %collective-permute-start.13 = (f32[128,256]{1,0:T(8,128)S(1)}, f32[128,256]{1,0:T(8,128)S(1)}, u32[]{:S(2)}, u32[]{:S(2)}) collective-permute-start(f32[128,256]{1,0:T(8,128)S(1)} %get-tuple-element.40), channel_id=1, source_target_pairs={{4,0},{5,1},{6,2},{7,3},{8,4},{9,5},{10,6},{11,7},{12,8},{13,9},{1... | collective-permute-start | bytes 393224 | tf_op jit(solution)/shard_map/ppermute | solution.py:168
  63.9 1.9 %collective-permute-start.14 = (f32[256,256]{1,0:T(8,128)}, f32[256,256]{1,0:T(8,128)}, u32[]{:S(2)}, u32[]{:S(2)}) collective-permute-start(f32[256,256]{1,0:T(8,128)} %pad_maximum_fusion.12), channel_id=1, source_target_pairs={{0,4},{1,5},{2,6},{3,7},{4,8},{5,9},{6,10},{7,11},{8,12},{9,13},{1... | collective-permute-start | bytes 786440 | tf_op jit(solution)/shard_map/ppermute | solution.py:169
  66.6 12.0 %collective-permute-done.13 = f32[128,256]{1,0:T(8,128)S(1)} collective-permute-done((f32[128,256]{1,0:T(8,128)S(1)}, f32[128,256]{1,0:T(8,128)S(1)}, u32[]{:S(2)}, u32[]{:S(2)}) %collective-permute-start.13) | collective-permute-done | bytes 131104 | tf_op jit(solution)/shard_map/ppermute | solution.py:168
  78.6 1.9 %collective-permute-start.16 = (f32[256,256]{1,0:T(8,128)}, f32[256,256]{1,0:T(8,128)}, u32[]{:S(2)}, u32[]{:S(2)}) collective-permute-start(f32[256,256]{1,0:T(8,128)} %pad_maximum_fusion.13), channel_id=1, source_target_pairs={{0,5},{1,6},{2,7},{3,8},{4,9},{5,10},{6,11},{7,12},{8,13},{9,14},{... | collective-permute-start | bytes 786440 | tf_op jit(solution)/shard_map/ppermute | solution.py:169
  81.2 1.9 %collective-permute-start.18 = (f32[256,256]{1,0:T(8,128)S(1)}, f32[256,256]{1,0:T(8,128)}, u32[]{:S(2)}, u32[]{:S(2)}) collective-permute-start(f32[256,256]{1,0:T(8,128)S(1)} %concatenate.58), channel_id=1, source_target_pairs={{0,6},{1,7},{2,8},{3,9},{4,10},{5,11},{6,12},{7,13},{8,14},{9,15},... | collective-permute-start | bytes 786440 | tf_op jit(solution)/shard_map/ppermute | solution.py:169
  85.1 4.2 %collective-permute-start.11 = (f32[128,256]{1,0:T(8,128)}, f32[128,256]{1,0:T(8,128)S(1)}, u32[]{:S(2)}, u32[]{:S(2)}) collective-permute-start(f32[128,256]{1,0:T(8,128)} %get-tuple-element.10), channel_id=1, source_target_pairs={{3,0},{4,1},{5,2},{6,3},{7,4},{8,5},{9,6},{10,7},{11,8},{12,9},{13... | collective-permute-start | bytes 393224 | tf_op jit(solution)/shard_map/ppermute | solution.py:168
  89.3 4.3 %collective-permute-start.15 = (f32[128,256]{1,0:T(8,128)}, f32[128,256]{1,0:T(8,128)S(1)}, u32[]{:S(2)}, u32[]{:S(2)}) collective-permute-start(f32[128,256]{1,0:T(8,128)} %get-tuple-element.11), channel_id=1, source_target_pairs={{5,0},{6,1},{7,2},{8,3},{9,4},{10,5},{11,6},{12,7},{13,8},{14,9},{... | collective-permute-start | bytes 393224 | tf_op jit(solution)/shard_map/ppermute | solution.py:168
  93.6 2.5 %collective-permute-start.17 = (f32[128,256]{1,0:T(8,128)}, f32[128,256]{1,0:T(8,128)S(1)}, u32[]{:S(2)}, u32[]{:S(2)}) collective-permute-start(f32[128,256]{1,0:T(8,128)} %get-tuple-element.16), channel_id=1, source_target_pairs={{6,0},{7,1},{8,2},{9,3},{10,4},{11,5},{12,6},{13,7},{14,8},{15,9},... | collective-permute-start | bytes 393224 | tf_op jit(solution)/shard_map/ppermute | solution.py:168
  96.1 7.0 %collective-permute-start.9 = (f32[128,256]{1,0:T(8,128)}, f32[128,256]{1,0:T(8,128)S(1)}, u32[]{:S(2)}, u32[]{:S(2)}) collective-permute-start(f32[128,256]{1,0:T(8,128)} %get-tuple-element.13), channel_id=1, source_target_pairs={{2,0},{3,1},{4,2},{5,3},{6,4},{7,5},{8,6},{9,7},{10,8},{11,9},{12,... | collective-permute-start | bytes 393224 | tf_op jit(solution)/shard_map/ppermute | solution.py:168
  103.1 1.9 %collective-permute-start.7 = (f32[128,256]{1,0:T(8,128)}, f32[128,256]{1,0:T(8,128)S(1)}, u32[]{:S(2)}, u32[]{:S(2)}) collective-permute-start(f32[128,256]{1,0:T(8,128)} %get-tuple-element.3), channel_id=1, source_target_pairs={{1,0},{2,1},{3,2},{4,3},{5,4},{6,5},{7,6},{8,7},{9,8},{10,9},{11,1... | collective-permute-start | bytes 393224 | tf_op jit(solution)/shard_map/ppermute | solution.py:168
  106.3 3.3 %collective-permute-done.7 = f32[128,256]{1,0:T(8,128)S(1)} collective-permute-done((f32[128,256]{1,0:T(8,128)}, f32[128,256]{1,0:T(8,128)S(1)}, u32[]{:S(2)}, u32[]{:S(2)}) %collective-permute-start.7) | collective-permute-done | bytes 131104 | tf_op jit(solution)/shard_map/ppermute | solution.py:168
  (87 shorter events, 25.7 us)
Async XLA Ops:
  4.3 3.9 %collective-permute-start = (bf16[2,128,256]{2,1,0:T(8,128)(2,1)S(1)}, bf16[2,128,256]{2,1,0:T(8,128)(2,1)S(1)}, u32[]{:S(2)}, u32[]{:S(2)}) collective-permute-start(bf16[2,128,256]{2,1,0:T(8,128)(2,1)S(1)} %pad_maximum_fusion.16), channel_id=1, source_target_pairs={{0,1},{1,0},{2,3},{3,2},{4,5},{5,4},{6,7},{7,6},{8,9},{9,8},{10,11... | collective-permute-start | bytes 393224 | tf_op jit(solution)/shard_map/ppermute | solution.py:46
  8.3 18.3 %collective-permute-start.1 = (bf16[2,128,256]{2,1,0:T(8,128)(2,1)S(1)}, bf16[2,128,256]{2,1,0:T(8,128)(2,1)S(1)}, u32[]{:S(2)}, u32[]{:S(2)}) collective-permute-start(bf16[2,128,256]{2,1,0:T(8,128)(2,1)S(1)} %pad_maximum_fusion.17), channel_id=1, source_target_pairs={{0,6},{1,7},{2,8},{3,9},{4,10},{5,11},{6,12},{7,13},{8,14},{9,15},... | collective-permute-start | bytes 393224 | tf_op jit(solution)/shard_map/ppermute | solution.py:55
  15.2 19.5 %collective-permute-start.4 = (bf16[4,128,256]{2,1,0:T(8,128)(2,1)S(1)}, bf16[4,128,256]{2,1,0:T(8,128)(2,1)S(1)}, u32[]{:S(2)}, u32[]{:S(2)}) collective-permute-start(bf16[4,128,256]{2,1,0:T(8,128)(2,1)S(1)} %pad_maximum_fusion.8), channel_id=1, source_target_pairs={{4,0},{5,1},{6,2},{7,3},{8,4},{9,5},{10,6},{11,7},{12,8},{13,9},{1... | collective-permute-start | bytes 786440 | tf_op jit(solution)/shard_map/ppermute | solution.py:56
  17.4 17.3 %collective-permute-start.5 = (bf16[4,128,256]{2,1,0:T(8,128)(2,1)S(1)}, bf16[4,128,256]{2,1,0:T(8,128)(2,1)S(1)}, u32[]{:S(2)}, u32[]{:S(2)}) collective-permute-start(bf16[4,128,256]{2,1,0:T(8,128)(2,1)S(1)} %pad_maximum_fusion.8), channel_id=1, source_target_pairs={{6,0},{7,1},{8,2},{9,3},{10,4},{11,5},{12,6},{13,7},{14,8},{15,9},... | collective-permute-start | bytes 786440 | tf_op jit(solution)/shard_map/ppermute | solution.py:56
  19.4 15.2 %collective-permute-start.2 = (bf16[2,128,256]{2,1,0:T(8,128)(2,1)S(1)}, bf16[2,128,256]{2,1,0:T(8,128)(2,1)S(1)}, u32[]{:S(2)}, u32[]{:S(2)}) collective-permute-start(bf16[2,128,256]{2,1,0:T(8,128)(2,1)S(1)} %pad_maximum_fusion.17), channel_id=1, source_target_pairs={{0,4},{1,5},{2,6},{3,7},{4,8},{5,9},{6,10},{7,11},{8,12},{9,13},{1... | collective-permute-start | bytes 393224 | tf_op jit(solution)/shard_map/ppermute | solution.py:55
  23.5 16.8 %collective-permute-start.6 = (bf16[4,128,256]{2,1,0:T(8,128)(2,1)S(1)}, bf16[4,128,256]{2,1,0:T(8,128)(2,1)S(1)}, u32[]{:S(2)}, u32[]{:S(2)}) collective-permute-start(bf16[4,128,256]{2,1,0:T(8,128)(2,1)S(1)} %pad_maximum_fusion.8), channel_id=1, source_target_pairs={{2,0},{3,1},{4,2},{5,3},{6,4},{7,5},{8,6},{9,7},{10,8},{11,9},{12,... | collective-permute-start | bytes 786440 | tf_op jit(solution)/shard_map/ppermute | solution.py:56
  26.5 13.8 %collective-permute-start.3 = (bf16[2,128,256]{2,1,0:T(8,128)(2,1)S(1)}, bf16[2,128,256]{2,1,0:T(8,128)(2,1)S(1)}, u32[]{:S(2)}, u32[]{:S(2)}) collective-permute-start(bf16[2,128,256]{2,1,0:T(8,128)(2,1)S(1)} %pad_maximum_fusion.17), channel_id=1, source_target_pairs={{0,2},{1,3},{2,4},{3,5},{4,6},{5,7},{6,8},{7,9},{8,10},{9,11},{10,... | collective-permute-start | bytes 393224 | tf_op jit(solution)/shard_map/ppermute | solution.py:55
  51.6 28.8 %collective-permute-start.8 = (f32[256,256]{1,0:T(8,128)S(1)}, f32[256,256]{1,0:T(8,128)S(1)}, u32[]{:S(2)}, u32[]{:S(2)}) collective-permute-start(f32[256,256]{1,0:T(8,128)S(1)} %pad_maximum_fusion.9), channel_id=1, source_target_pairs={{0,1},{1,2},{2,3},{3,4},{4,5},{5,6},{6,7},{7,8},{8,9},{9,10},{10,1... | collective-permute-start | bytes 786440 | tf_op jit(solution)/shard_map/ppermute | solution.py:169
  54.4 30.7 %collective-permute-start.10 = (f32[256,256]{1,0:T(8,128)}, f32[256,256]{1,0:T(8,128)}, u32[]{:S(2)}, u32[]{:S(2)}) collective-permute-start(f32[256,256]{1,0:T(8,128)} %pad_maximum_fusion.10), channel_id=1, source_target_pairs={{0,2},{1,3},{2,4},{3,5},{4,6},{5,7},{6,8},{7,9},{8,10},{9,11},{10,... | collective-permute-start | bytes 786440 | tf_op jit(solution)/shard_map/ppermute | solution.py:169
  56.3 32.9 %collective-permute-start.12 = (f32[256,256]{1,0:T(8,128)S(1)}, f32[256,256]{1,0:T(8,128)}, u32[]{:S(2)}, u32[]{:S(2)}) collective-permute-start(f32[256,256]{1,0:T(8,128)S(1)} %pad_maximum_fusion.11), channel_id=1, source_target_pairs={{0,3},{1,4},{2,5},{3,6},{4,7},{5,8},{6,9},{7,10},{8,11},{9,12},{10... | collective-permute-start | bytes 786440 | tf_op jit(solution)/shard_map/ppermute | solution.py:169
  58.3 20.3 %collective-permute-start.13 = (f32[128,256]{1,0:T(8,128)S(1)}, f32[128,256]{1,0:T(8,128)S(1)}, u32[]{:S(2)}, u32[]{:S(2)}) collective-permute-start(f32[128,256]{1,0:T(8,128)S(1)} %get-tuple-element.40), channel_id=1, source_target_pairs={{4,0},{5,1},{6,2},{7,3},{8,4},{9,5},{10,6},{11,7},{12,8},{13,9},{1... | collective-permute-start | bytes 393224 | tf_op jit(solution)/shard_map/ppermute | solution.py:168
  63.9 29.6 %collective-permute-start.14 = (f32[256,256]{1,0:T(8,128)}, f32[256,256]{1,0:T(8,128)}, u32[]{:S(2)}, u32[]{:S(2)}) collective-permute-start(f32[256,256]{1,0:T(8,128)} %pad_maximum_fusion.12), channel_id=1, source_target_pairs={{0,4},{1,5},{2,6},{3,7},{4,8},{5,9},{6,10},{7,11},{8,12},{9,13},{1... | collective-permute-start | bytes 786440 | tf_op jit(solution)/shard_map/ppermute | solution.py:169
  78.6 1.9 %copy-start.1 = (f32[128,256]{1,0:T(8,128)}, f32[128,256]{1,0:T(8,128)S(1)}, u32[]{:S(2)}) copy-start(f32[128,256]{1,0:T(8,128)S(1)} %collective-permute-done.13) | copy-start | bytes 393220
  78.6 17.5 %collective-permute-start.16 = (f32[256,256]{1,0:T(8,128)}, f32[256,256]{1,0:T(8,128)}, u32[]{:S(2)}, u32[]{:S(2)}) collective-permute-start(f32[256,256]{1,0:T(8,128)} %pad_maximum_fusion.13), channel_id=1, source_target_pairs={{0,5},{1,6},{2,7},{3,8},{4,9},{5,10},{6,11},{7,12},{8,13},{9,14},{... | collective-permute-start | bytes 786440 | tf_op jit(solution)/shard_map/ppermute | solution.py:169
  80.5 0.7 copy-start
  81.2 21.9 %collective-permute-start.18 = (f32[256,256]{1,0:T(8,128)S(1)}, f32[256,256]{1,0:T(8,128)}, u32[]{:S(2)}, u32[]{:S(2)}) collective-permute-start(f32[256,256]{1,0:T(8,128)S(1)} %concatenate.58), channel_id=1, source_target_pairs={{0,6},{1,7},{2,8},{3,9},{4,10},{5,11},{6,12},{7,13},{8,14},{9,15},... | collective-permute-start | bytes 786440 | tf_op jit(solution)/shard_map/ppermute | solution.py:169
  85.1 21.2 %collective-permute-start.11 = (f32[128,256]{1,0:T(8,128)}, f32[128,256]{1,0:T(8,128)S(1)}, u32[]{:S(2)}, u32[]{:S(2)}) collective-permute-start(f32[128,256]{1,0:T(8,128)} %get-tuple-element.10), channel_id=1, source_target_pairs={{3,0},{4,1},{5,2},{6,3},{7,4},{8,5},{9,6},{10,7},{11,8},{12,9},{13... | collective-permute-start | bytes 393224 | tf_op jit(solution)/shard_map/ppermute | solution.py:168
  89.3 17.0 %collective-permute-start.15 = (f32[128,256]{1,0:T(8,128)}, f32[128,256]{1,0:T(8,128)S(1)}, u32[]{:S(2)}, u32[]{:S(2)}) collective-permute-start(f32[128,256]{1,0:T(8,128)} %get-tuple-element.11), channel_id=1, source_target_pairs={{5,0},{6,1},{7,2},{8,3},{9,4},{10,5},{11,6},{12,7},{13,8},{14,9},{... | collective-permute-start | bytes 393224 | tf_op jit(solution)/shard_map/ppermute | solution.py:168
  93.6 12.8 %collective-permute-start.17 = (f32[128,256]{1,0:T(8,128)}, f32[128,256]{1,0:T(8,128)S(1)}, u32[]{:S(2)}, u32[]{:S(2)}) collective-permute-start(f32[128,256]{1,0:T(8,128)} %get-tuple-element.16), channel_id=1, source_target_pairs={{6,0},{7,1},{8,2},{9,3},{10,4},{11,5},{12,6},{13,7},{14,8},{15,9},... | collective-permute-start | bytes 393224 | tf_op jit(solution)/shard_map/ppermute | solution.py:168
  96.1 10.3 %collective-permute-start.9 = (f32[128,256]{1,0:T(8,128)}, f32[128,256]{1,0:T(8,128)S(1)}, u32[]{:S(2)}, u32[]{:S(2)}) collective-permute-start(f32[128,256]{1,0:T(8,128)} %get-tuple-element.13), channel_id=1, source_target_pairs={{2,0},{3,1},{4,2},{5,3},{6,4},{7,5},{8,6},{9,7},{10,8},{11,9},{12,... | collective-permute-start | bytes 393224 | tf_op jit(solution)/shard_map/ppermute | solution.py:168
  103.1 6.5 %collective-permute-start.7 = (f32[128,256]{1,0:T(8,128)}, f32[128,256]{1,0:T(8,128)S(1)}, u32[]{:S(2)}, u32[]{:S(2)}) collective-permute-start(f32[128,256]{1,0:T(8,128)} %get-tuple-element.3), channel_id=1, source_target_pairs={{1,0},{2,1},{3,2},{4,3},{5,4},{6,5},{7,6},{8,7},{9,8},{10,9},{11,1... | collective-permute-start | bytes 393224 | tf_op jit(solution)/shard_map/ppermute | solution.py:168
where the time goes:
time: 113 us; the launch traced here: 112 us
  starting transfers between devices  54.7 us (48%)
  waiting for transfers between devices  26.7 us (24%)
  other arithmetic  14.2 us (13%)
  local copies, waits for them, and re-layouts  8.35 us (7%)
  matrix products  6.53 us (6%)
  between operations  1.96 us (2%)
    ppermute x6, starting transfers between devices, on_device(): sent_low = lax.ppermute(low_parts[REACH - k] + to_below[k - 1], AXES, up)  24.8 us
    ppermute x6, waiting for transfers between devices, on_device(): sent_low = lax.ppermute(low_parts[REACH - k] + to_below[k - 1], AXES, up)  15.3 us
    ppermute x6, starting transfers between devices, on_device(): lax.ppermute(jnp.concatenate([to_above_low[k - 1], to_high[k - 1]], 0), A...  11.5 us
    ppermute x3, waiting for transfers between devices, on_device(): below_chip = lax.ppermute(chip[:2], AXES, up)  11.4 us
    ppermute x3, starting transfers between devices, on_device(): below_chip = lax.ppermute(chip[:2], AXES, up)  10.4 us
    ppermute x3, starting transfers between devices, on_device(): above_chip = lax.ppermute(chip, AXES, down)  7.25 us
    another operation x2, other arithmetic, on_device(): grad_kv = jnp.stack([grad_low, grad_high])  2.63 us
  transfers between devices with their start and end apart: 19, of which 4 were waited for; matrix products, arithmetic and copies ran while one was open for 10% of the time, Pallas kernels for 0%

commit v1 on v0

--- a/solution.py
+++ b/solution.py
@@ -33,16 +33,15 @@
     span = REACH + 1
 
     first_slot = jnp.where(block_order[2 * device] < count, 0, 1).astype(jnp.int32)
-    second_slot = 1 - first_slot
 
-    def take_block(rows, slot):
-        return lax.dynamic_slice_in_dim(rows, slot * length, length, 0)
+    swapped = first_slot == 1
 
-    joined = jnp.concatenate([key_states, value_states], 1)
-    low = take_block(joined, first_slot)
-    high = take_block(joined, second_slot)
+    def in_sequence_order(rows):
+        paired = rows.reshape((2, length) + rows.shape[1:])
+        return jnp.where(swapped, paired[::-1], paired)
+
+    own = in_sequence_order(jnp.concatenate([key_states, value_states], 1))
     odd = (device % 2) == 1
-    own = jnp.stack([low, high])
     mate = lax.ppermute(own, AXES, [(s, s ^ 1) for s in range(count)])
     even_part = jnp.where(odd, mate, own)
     odd_part = jnp.where(odd, own, mate)
@@ -81,18 +80,9 @@
     key_window = windows[..., :head_size]
     value_window = windows[..., head_size:]
 
-    def split_heads(rows):
-        return rows.reshape(rows.shape[0], rows.shape[1] // head_size, head_size)
-
-    query_pair = jnp.stack(
-        [split_heads(take_block(queries, first_slot)), split_heads(take_block(queries, second_slot))]
-    )
-    output_pair = jnp.stack(
-        [
-            split_heads(take_block(grad_output, first_slot)),
-            split_heads(take_block(grad_output, second_slot)),
-        ]
-    )
+    heads = queries.shape[1] // head_size
+    query_pair = in_sequence_order(queries).reshape(2, length, heads, head_size)
+    output_pair = in_sequence_order(grad_output).reshape(2, length, heads, head_size)
 
     pad = REACH * length
     padded_documents = jnp.concatenate([jnp.full((pad,), -1, documents.dtype), documents])
@@ -181,7 +171,7 @@
     grad_values = grad_kv[:, :, head_size:].astype(jnp.bfloat16)
 
     def restore(paired):
-        return jnp.concatenate([paired[first_slot], paired[second_slot]], 0)
+        return jnp.where(swapped, paired[::-1], paired).reshape((2 * length,) + paired.shape[2:])
 
     return (restore(grad_query), restore(grad_keys), restore(grad_values))
 

time: 113 us -> 110 us (0.973)
  local copies, waits for them, and re-layouts: 8.35 us -> 6.52 us
    reshape x0 -> x2, local copies, waits for them, and re-layouts: none -> 2.63 us  [in_sequence_order(): paired = rows.reshape((2, length) + rows.shape[1:])]
    unnamed x9 -> x4, local copies, waits for them, and re-layouts: 2.23 us -> 0.01 us
    select_n x0 -> x5, other arithmetic: none -> 1.63 us  [the longest x3 1.4 us: restore(): jnp.where(swapped, paired[::-1], paired)]
    dynamic_slice x4 -> x0, local copies, waits for them, and re-layouts: 1.6 us -> none  [the longest x1 1.27 us: take_block(): return lax.dynamic_slice_in_dim(rows, slot * length, length, 0)]
    concatenate x3 -> x1, other arithmetic: 2.1 us -> 0.89 us  [on_device(): own = in_sequence_order(jnp.concatenate([key_states, value_states], 1))]
where the time goes in v1:
time: 110 us; the launch traced here: 109 us
  starting transfers between devices  54.7 us (50%)
  waiting for transfers between devices  26.4 us (24%)
  other arithmetic  13.3 us (12%)
  local copies, waits for them, and re-layouts  6.52 us (6%)
  matrix products  6.5 us (6%)
  between operations  1.92 us (2%)
    ppermute x6, starting transfers between devices, on_device(): sent_low = lax.ppermute(low_parts[REACH - k] + to_below[k - 1], AXES, up)  24.8 us
    ppermute x6, waiting for transfers between devices, on_device(): sent_low = lax.ppermute(low_parts[REACH - k] + to_below[k - 1], AXES, up)  15 us
    ppermute x6, starting transfers between devices, on_device(): lax.ppermute(jnp.concatenate([to_above_low[k - 1], to_high[k - 1]], 0), A...  11.5 us
    ppermute x3, waiting for transfers between devices, on_device(): below_chip = lax.ppermute(chip[:2], AXES, up)  11.4 us
    ppermute x3, starting transfers between devices, on_device(): below_chip = lax.ppermute(chip[:2], AXES, up)  10.4 us
    ppermute x3, starting transfers between devices, on_device(): above_chip = lax.ppermute(chip, AXES, down)  7.25 us
    another operation x2, other arithmetic, on_device(): grad_kv = jnp.stack([grad_low, grad_high])  2.63 us
    reshape x2, local copies, waits for them, and re-layouts, in_sequence_order(): paired = rows.reshape((2, length) + rows.shape[1:])  2.63 us
  transfers between devices with their start and end apart: 19, of which 4 were waited for; matrix products, arithmetic and copies ran while one was open for 10% of the time, Pallas kernels for 0%

profile of v1, /device:TPU:21, one launch (start us, length us, event | category | flops | bytes accessed | tf_op | source)
XLA Modules:
  0.0 109.4 jit_solution(5996703640890128633)
XLA Ops:
  8.9 4.1 %collective-permute-start.1 = (bf16[2,128,256]{2,1,0:T(8,128)(2,1)S(1)}, bf16[2,128,256]{2,1,0:T(8,128)(2,1)S(1)}, u32[]{:S(2)}, u32[]{:S(2)}) collective-permute-start(bf16[2,128,256]{2,1,0:T(8,128)(2,1)S(1)} %pad_maximum_fusion.10), channel_id=1, source_target_pairs={{0,6},{1,7},{2,8},{3,9},{4,10},{5,11},{6,12},{7,13},{8,14},{9,15},... | collective-permute-start | bytes 393224 | tf_op jit(solution)/shard_map/ppermute | solution.py:54
  14.5 2.1 %collective-permute-start.4 = (bf16[4,128,256]{2,1,0:T(8,128)(2,1)S(1)}, bf16[4,128,256]{2,1,0:T(8,128)(2,1)S(1)}, u32[]{:S(2)}, u32[]{:S(2)}) collective-permute-start(bf16[4,128,256]{2,1,0:T(8,128)(2,1)S(1)} %pad_maximum_fusion.1), channel_id=1, source_target_pairs={{4,0},{5,1},{6,2},{7,3},{8,4},{9,5},{10,6},{11,7},{12,8},{13,9},{1... | collective-permute-start | bytes 786440 | tf_op jit(solution)/shard_map/ppermute | solution.py:55
  16.7 2.0 %collective-permute-start.5 = (bf16[4,128,256]{2,1,0:T(8,128)(2,1)S(1)}, bf16[4,128,256]{2,1,0:T(8,128)(2,1)S(1)}, u32[]{:S(2)}, u32[]{:S(2)}) collective-permute-start(bf16[4,128,256]{2,1,0:T(8,128)(2,1)S(1)} %pad_maximum_fusion.1), channel_id=1, source_target_pairs={{6,0},{7,1},{8,2},{9,3},{10,4},{11,5},{12,6},{13,7},{14,8},{15,9},... | collective-permute-start | bytes 786440 | tf_op jit(solution)/shard_map/ppermute | solution.py:55
  18.7 4.0 %collective-permute-start.2 = (bf16[2,128,256]{2,1,0:T(8,128)(2,1)S(1)}, bf16[2,128,256]{2,1,0:T(8,128)(2,1)S(1)}, u32[]{:S(2)}, u32[]{:S(2)}) collective-permute-start(bf16[2,128,256]{2,1,0:T(8,128)(2,1)S(1)} %pad_maximum_fusion.10), channel_id=1, source_target_pairs={{0,4},{1,5},{2,6},{3,7},{4,8},{5,9},{6,10},{7,11},{8,12},{9,13},{1... | collective-permute-start | bytes 393224 | tf_op jit(solution)/shard_map/ppermute | solution.py:54
  22.8 3.1 %collective-permute-start.6 = (bf16[4,128,256]{2,1,0:T(8,128)(2,1)S(1)}, bf16[4,128,256]{2,1,0:T(8,128)(2,1)S(1)}, u32[]{:S(2)}, u32[]{:S(2)}) collective-permute-start(bf16[4,128,256]{2,1,0:T(8,128)(2,1)S(1)} %pad_maximum_fusion.1), channel_id=1, source_target_pairs={{2,0},{3,1},{4,2},{5,3},{6,4},{7,5},{8,6},{9,7},{10,8},{11,9},{12,... | collective-permute-start | bytes 786440 | tf_op jit(solution)/shard_map/ppermute | solution.py:55
  25.9 2.2 %collective-permute-start.3 = (bf16[2,128,256]{2,1,0:T(8,128)(2,1)S(1)}, bf16[2,128,256]{2,1,0:T(8,128)(2,1)S(1)}, u32[]{:S(2)}, u32[]{:S(2)}) collective-permute-start(bf16[2,128,256]{2,1,0:T(8,128)(2,1)S(1)} %pad_maximum_fusion.10), channel_id=1, source_target_pairs={{0,2},{1,3},{2,4},{3,5},{4,6},{5,7},{6,8},{7,9},{8,10},{9,11},{10,... | collective-permute-start | bytes 393224 | tf_op jit(solution)/shard_map/ppermute | solution.py:54
  28.1 5.9 %collective-permute-done.2 = bf16[2,128,256]{2,1,0:T(8,128)(2,1)S(1)} collective-permute-done((bf16[2,128,256]{2,1,0:T(8,128)(2,1)S(1)}, bf16[2,128,256]{2,1,0:T(8,128)(2,1)S(1)}, u32[]{:S(2)}, u32[]{:S(2)}) %collective-permute-start.2) | collective-permute-done | bytes 131104 | tf_op jit(solution)/shard_map/ppermute | solution.py:54
  34.1 5.5 %collective-permute-done.3 = bf16[2,128,256]{2,1,0:T(8,128)(2,1)S(1)} collective-permute-done((bf16[2,128,256]{2,1,0:T(8,128)(2,1)S(1)}, bf16[2,128,256]{2,1,0:T(8,128)(2,1)S(1)}, u32[]{:S(2)}, u32[]{:S(2)}) %collective-permute-start.3) | collective-permute-done | bytes 131104 | tf_op jit(solution)/shard_map/ppermute | solution.py:54
  42.7 2.0 %fusion = (f32[2,8,128]{2,1,0:T(8,128)S(1)}, f32[2,896,128,8]{2,1,3,0:T(8,128)S(1)}) fusion(f32[2,896,128,8]{2,1,3,0:T(8,128)S(1)} %get-tuple-element.49, f32[2,8,128]{2,1,0:T(8,128)S(1)} %log_add_fusion, pred[2,128,896]{1,2,0:T(8,128)(4,1)S(1)} %compare_and_fusion, bf16[2,128,8,128]{1,3,2,0:T(8,128)(2,1)S(1)} %bitcast.244, ...), kind=kOutput, calls=%fused_computation.2 | convolution fusion | flops 479852544 | bytes 16367616 | tf_op jit(solution)/shard_map/qbhd,qwd->qhbw/dot_general | solution.py:110
  46.1 2.1 %fusion.2 = bf16[2,8,128,896]{2,3,1,0:T(8,128)(2,1)S(1)} fusion(f32[2,896,128,8]{2,1,3,0:T(8,128)S(1)} %get-tuple-element.51, f32[2,896,128,8]{2,1,3,0:T(8,128)S(1)} %get-tuple-element.49, f32[2,8,128]{2,1,0:T(8,128)S(1)} %get-tuple-element.50, f32[2,8,128]{2,1,0:T(8,128)S(1)} %log_add_fusion, pred[2,128,896]{1,2,0:T(8,128)(4,1)S(1)} %compare_and_fusion), kind=kLoop, calls=%fused_computation.4 | loop fusion | flops 11010048 | bytes 18595840 | tf_op jit(solution)/shard_map/convert_element_type | solution.py:121
  50.3 1.9 %collective-permute-start.8 = (f32[256,256]{1,0:T(8,128)S(1)}, f32[256,256]{1,0:T(8,128)S(1)}, u32[]{:S(2)}, u32[]{:S(2)}) collective-permute-start(f32[256,256]{1,0:T(8,128)S(1)} %pad_maximum_fusion.2), channel_id=1, source_target_pairs={{0,1},{1,2},{2,3},{3,4},{4,5},{5,6},{6,7},{7,8},{8,9},{9,10},{10,1... | collective-permute-start | bytes 786440 | tf_op jit(solution)/shard_map/ppermute | solution.py:159
  52.3 1.9 %collective-permute-start.10 = (f32[256,256]{1,0:T(8,128)S(1)}, f32[256,256]{1,0:T(8,128)}, u32[]{:S(2)}, u32[]{:S(2)}) collective-permute-start(f32[256,256]{1,0:T(8,128)S(1)} %pad_maximum_fusion.3), channel_id=1, source_target_pairs={{0,2},{1,3},{2,4},{3,5},{4,6},{5,7},{6,8},{7,9},{8,10},{9,11},{10,... | collective-permute-start | bytes 786440 | tf_op jit(solution)/shard_map/ppermute | solution.py:159
  54.3 1.9 %collective-permute-start.12 = (f32[256,256]{1,0:T(8,128)S(1)}, f32[256,256]{1,0:T(8,128)}, u32[]{:S(2)}, u32[]{:S(2)}) collective-permute-start(f32[256,256]{1,0:T(8,128)S(1)} %pad_maximum_fusion.4), channel_id=1, source_target_pairs={{0,3},{1,4},{2,5},{3,6},{4,7},{5,8},{6,9},{7,10},{8,11},{9,12},{10... | collective-permute-start | bytes 786440 | tf_op jit(solution)/shard_map/ppermute | solution.py:159
  56.2 4.9 %collective-permute-start.13 = (f32[128,256]{1,0:T(8,128)S(1)}, f32[128,256]{1,0:T(8,128)S(1)}, u32[]{:S(2)}, u32[]{:S(2)}) collective-permute-start(f32[128,256]{1,0:T(8,128)S(1)} %get-tuple-element.34), channel_id=1, source_target_pairs={{4,0},{5,1},{6,2},{7,3},{8,4},{9,5},{10,6},{11,7},{12,8},{13,9},{1... | collective-permute-start | bytes 393224 | tf_op jit(solution)/shard_map/ppermute | solution.py:158
  61.9 1.9 %collective-permute-start.14 = (f32[256,256]{1,0:T(8,128)}, f32[256,256]{1,0:T(8,128)}, u32[]{:S(2)}, u32[]{:S(2)}) collective-permute-start(f32[256,256]{1,0:T(8,128)} %pad_maximum_fusion.5), channel_id=1, source_target_pairs={{0,4},{1,5},{2,6},{3,7},{4,8},{5,9},{6,10},{7,11},{8,12},{9,13},{1... | collective-permute-start | bytes 786440 | tf_op jit(solution)/shard_map/ppermute | solution.py:159
  64.6 12.0 %collective-permute-done.13 = f32[128,256]{1,0:T(8,128)S(1)} collective-permute-done((f32[128,256]{1,0:T(8,128)S(1)}, f32[128,256]{1,0:T(8,128)S(1)}, u32[]{:S(2)}, u32[]{:S(2)}) %collective-permute-start.13) | collective-permute-done | bytes 131104 | tf_op jit(solution)/shard_map/ppermute | solution.py:158
  76.5 1.9 %collective-permute-start.16 = (f32[256,256]{1,0:T(8,128)}, f32[256,256]{1,0:T(8,128)}, u32[]{:S(2)}, u32[]{:S(2)}) collective-permute-start(f32[256,256]{1,0:T(8,128)} %pad_maximum_fusion.6), channel_id=1, source_target_pairs={{0,5},{1,6},{2,7},{3,8},{4,9},{5,10},{6,11},{7,12},{8,13},{9,14},{... | collective-permute-start | bytes 786440 | tf_op jit(solution)/shard_map/ppermute | solution.py:159
  78.5 1.9 %collective-permute-start.18 = (f32[256,256]{1,0:T(8,128)S(1)}, f32[256,256]{1,0:T(8,128)}, u32[]{:S(2)}, u32[]{:S(2)}) collective-permute-start(f32[256,256]{1,0:T(8,128)S(1)} %concatenate.48), channel_id=1, source_target_pairs={{0,6},{1,7},{2,8},{3,9},{4,10},{5,11},{6,12},{7,13},{8,14},{9,15},... | collective-permute-start | bytes 786440 | tf_op jit(solution)/shard_map/ppermute | solution.py:159
  82.3 4.7 %collective-permute-start.11 = (f32[128,256]{1,0:T(8,128)}, f32[128,256]{1,0:T(8,128)S(1)}, u32[]{:S(2)}, u32[]{:S(2)}) collective-permute-start(f32[128,256]{1,0:T(8,128)} %get-tuple-element.10), channel_id=1, source_target_pairs={{3,0},{4,1},{5,2},{6,3},{7,4},{8,5},{9,6},{10,7},{11,8},{12,9},{13... | collective-permute-start | bytes 393224 | tf_op jit(solution)/shard_map/ppermute | solution.py:158
  87.1 4.3 %collective-permute-start.15 = (f32[128,256]{1,0:T(8,128)}, f32[128,256]{1,0:T(8,128)S(1)}, u32[]{:S(2)}, u32[]{:S(2)}) collective-permute-start(f32[128,256]{1,0:T(8,128)} %get-tuple-element.11), channel_id=1, source_target_pairs={{5,0},{6,1},{7,2},{8,3},{9,4},{10,5},{11,6},{12,7},{13,8},{14,9},{... | collective-permute-start | bytes 393224 | tf_op jit(solution)/shard_map/ppermute | solution.py:158
  91.3 1.9 %collective-permute-start.17 = (f32[128,256]{1,0:T(8,128)}, f32[128,256]{1,0:T(8,128)S(1)}, u32[]{:S(2)}, u32[]{:S(2)}) collective-permute-start(f32[128,256]{1,0:T(8,128)} %get-tuple-element.16), channel_id=1, source_target_pairs={{6,0},{7,1},{8,2},{9,3},{10,4},{11,5},{12,6},{13,7},{14,8},{15,9},... | collective-permute-start | bytes 393224 | tf_op jit(solution)/shard_map/ppermute | solution.py:158
  93.3 7.0 %collective-permute-start.9 = (f32[128,256]{1,0:T(8,128)}, f32[128,256]{1,0:T(8,128)S(1)}, u32[]{:S(2)}, u32[]{:S(2)}) collective-permute-start(f32[128,256]{1,0:T(8,128)} %get-tuple-element.13), channel_id=1, source_target_pairs={{2,0},{3,1},{4,2},{5,3},{6,4},{7,5},{8,6},{9,7},{10,8},{11,9},{12,... | collective-permute-start | bytes 393224 | tf_op jit(solution)/shard_map/ppermute | solution.py:158
  100.4 1.9 %collective-permute-start.7 = (f32[128,256]{1,0:T(8,128)S(1)}, f32[128,256]{1,0:T(8,128)S(1)}, u32[]{:S(2)}, u32[]{:S(2)}) collective-permute-start(f32[128,256]{1,0:T(8,128)S(1)} %get-tuple-element.3), channel_id=1, source_target_pairs={{1,0},{2,1},{3,2},{4,3},{5,4},{6,5},{7,6},{8,7},{9,8},{10,9},{11,1... | collective-permute-start | bytes 393224 | tf_op jit(solution)/shard_map/ppermute | solution.py:158
  103.6 3.1 %collective-permute-done.7 = f32[128,256]{1,0:T(8,128)S(1)} collective-permute-done((f32[128,256]{1,0:T(8,128)S(1)}, f32[128,256]{1,0:T(8,128)S(1)}, u32[]{:S(2)}, u32[]{:S(2)}) %collective-permute-start.7) | collective-permute-done | bytes 131104 | tf_op jit(solution)/shard_map/ppermute | solution.py:158
  (75 shorter events, 23.0 us)
Async XLA Ops:
  3.5 5.3 %collective-permute-start = (bf16[2,128,256]{2,1,0:T(8,128)(2,1)S(1)}, bf16[2,128,256]{2,1,0:T(8,128)(2,1)S(1)}, u32[]{:S(2)}, u32[]{:S(2)}) collective-permute-start(bf16[2,128,256]{2,1,0:T(8,128)(2,1)S(1)} %reverse_select_fusion.3), channel_id=1, source_target_pairs={{0,1},{1,0},{2,3},{3,2},{4,5},{5,4},{6,7},{7,6},{8,9},{9,8},{10,11... | collective-permute-start | bytes 393224 | tf_op jit(solution)/shard_map/ppermute | solution.py:45
  8.9 17.0 %collective-permute-start.1 = (bf16[2,128,256]{2,1,0:T(8,128)(2,1)S(1)}, bf16[2,128,256]{2,1,0:T(8,128)(2,1)S(1)}, u32[]{:S(2)}, u32[]{:S(2)}) collective-permute-start(bf16[2,128,256]{2,1,0:T(8,128)(2,1)S(1)} %pad_maximum_fusion.10), channel_id=1, source_target_pairs={{0,6},{1,7},{2,8},{3,9},{4,10},{5,11},{6,12},{7,13},{8,14},{9,15},... | collective-permute-start | bytes 393224 | tf_op jit(solution)/shard_map/ppermute | solution.py:54
  14.5 19.5 %collective-permute-start.4 = (bf16[4,128,256]{2,1,0:T(8,128)(2,1)S(1)}, bf16[4,128,256]{2,1,0:T(8,128)(2,1)S(1)}, u32[]{:S(2)}, u32[]{:S(2)}) collective-permute-start(bf16[4,128,256]{2,1,0:T(8,128)(2,1)S(1)} %pad_maximum_fusion.1), channel_id=1, source_target_pairs={{4,0},{5,1},{6,2},{7,3},{8,4},{9,5},{10,6},{11,7},{12,8},{13,9},{1... | collective-permute-start | bytes 786440 | tf_op jit(solution)/shard_map/ppermute | solution.py:55
  16.7 17.3 %collective-permute-start.5 = (bf16[4,128,256]{2,1,0:T(8,128)(2,1)S(1)}, bf16[4,128,256]{2,1,0:T(8,128)(2,1)S(1)}, u32[]{:S(2)}, u32[]{:S(2)}) collective-permute-start(bf16[4,128,256]{2,1,0:T(8,128)(2,1)S(1)} %pad_maximum_fusion.1), channel_id=1, source_target_pairs={{6,0},{7,1},{8,2},{9,3},{10,4},{11,5},{12,6},{13,7},{14,8},{15,9},... | collective-permute-start | bytes 786440 | tf_op jit(solution)/shard_map/ppermute | solution.py:55
  18.7 15.2 %collective-permute-start.2 = (bf16[2,128,256]{2,1,0:T(8,128)(2,1)S(1)}, bf16[2,128,256]{2,1,0:T(8,128)(2,1)S(1)}, u32[]{:S(2)}, u32[]{:S(2)}) collective-permute-start(bf16[2,128,256]{2,1,0:T(8,128)(2,1)S(1)} %pad_maximum_fusion.10), channel_id=1, source_target_pairs={{0,4},{1,5},{2,6},{3,7},{4,8},{5,9},{6,10},{7,11},{8,12},{9,13},{1... | collective-permute-start | bytes 393224 | tf_op jit(solution)/shard_map/ppermute | solution.py:54
  22.8 16.8 %collective-permute-start.6 = (bf16[4,128,256]{2,1,0:T(8,128)(2,1)S(1)}, bf16[4,128,256]{2,1,0:T(8,128)(2,1)S(1)}, u32[]{:S(2)}, u32[]{:S(2)}) collective-permute-start(bf16[4,128,256]{2,1,0:T(8,128)(2,1)S(1)} %pad_maximum_fusion.1), channel_id=1, source_target_pairs={{2,0},{3,1},{4,2},{5,3},{6,4},{7,5},{8,6},{9,7},{10,8},{11,9},{12,... | collective-permute-start | bytes 786440 | tf_op jit(solution)/shard_map/ppermute | solution.py:55
  25.9 13.8 %collective-permute-start.3 = (bf16[2,128,256]{2,1,0:T(8,128)(2,1)S(1)}, bf16[2,128,256]{2,1,0:T(8,128)(2,1)S(1)}, u32[]{:S(2)}, u32[]{:S(2)}) collective-permute-start(bf16[2,128,256]{2,1,0:T(8,128)(2,1)S(1)} %pad_maximum_fusion.10), channel_id=1, source_target_pairs={{0,2},{1,3},{2,4},{3,5},{4,6},{5,7},{6,8},{7,9},{8,10},{9,11},{10,... | collective-permute-start | bytes 393224 | tf_op jit(solution)/shard_map/ppermute | solution.py:54
  50.3 28.1 %collective-permute-start.8 = (f32[256,256]{1,0:T(8,128)S(1)}, f32[256,256]{1,0:T(8,128)S(1)}, u32[]{:S(2)}, u32[]{:S(2)}) collective-permute-start(f32[256,256]{1,0:T(8,128)S(1)} %pad_maximum_fusion.2), channel_id=1, source_target_pairs={{0,1},{1,2},{2,3},{3,4},{4,5},{5,6},{6,7},{7,8},{8,9},{9,10},{10,1... | collective-permute-start | bytes 786440 | tf_op jit(solution)/shard_map/ppermute | solution.py:159
  52.3 30.0 %collective-permute-start.10 = (f32[256,256]{1,0:T(8,128)S(1)}, f32[256,256]{1,0:T(8,128)}, u32[]{:S(2)}, u32[]{:S(2)}) collective-permute-start(f32[256,256]{1,0:T(8,128)S(1)} %pad_maximum_fusion.3), channel_id=1, source_target_pairs={{0,2},{1,3},{2,4},{3,5},{4,6},{5,7},{6,8},{7,9},{8,10},{9,11},{10,... | collective-permute-start | bytes 786440 | tf_op jit(solution)/shard_map/ppermute | solution.py:159
  54.3 32.8 %collective-permute-start.12 = (f32[256,256]{1,0:T(8,128)S(1)}, f32[256,256]{1,0:T(8,128)}, u32[]{:S(2)}, u32[]{:S(2)}) collective-permute-start(f32[256,256]{1,0:T(8,128)S(1)} %pad_maximum_fusion.4), channel_id=1, source_target_pairs={{0,3},{1,4},{2,5},{3,6},{4,7},{5,8},{6,9},{7,10},{8,11},{9,12},{10... | collective-permute-start | bytes 786440 | tf_op jit(solution)/shard_map/ppermute | solution.py:159
  56.2 20.3 %collective-permute-start.13 = (f32[128,256]{1,0:T(8,128)S(1)}, f32[128,256]{1,0:T(8,128)S(1)}, u32[]{:S(2)}, u32[]{:S(2)}) collective-permute-start(f32[128,256]{1,0:T(8,128)S(1)} %get-tuple-element.34), channel_id=1, source_target_pairs={{4,0},{5,1},{6,2},{7,3},{8,4},{9,5},{10,6},{11,7},{12,8},{13,9},{1... | collective-permute-start | bytes 393224 | tf_op jit(solution)/shard_map/ppermute | solution.py:158
  61.9 29.4 %collective-permute-start.14 = (f32[256,256]{1,0:T(8,128)}, f32[256,256]{1,0:T(8,128)}, u32[]{:S(2)}, u32[]{:S(2)}) collective-permute-start(f32[256,256]{1,0:T(8,128)} %pad_maximum_fusion.5), channel_id=1, source_target_pairs={{0,4},{1,5},{2,6},{3,7},{4,8},{5,9},{6,10},{7,11},{8,12},{9,13},{1... | collective-permute-start | bytes 786440 | tf_op jit(solution)/shard_map/ppermute | solution.py:159
  76.5 4.7 %copy-start.1 = (f32[128,256]{1,0:T(8,128)}, f32[128,256]{1,0:T(8,128)S(1)}, u32[]{:S(2)}) copy-start(f32[128,256]{1,0:T(8,128)S(1)} %collective-permute-done.13) | copy-start | bytes 393220
  76.5 16.8 %collective-permute-start.16 = (f32[256,256]{1,0:T(8,128)}, f32[256,256]{1,0:T(8,128)}, u32[]{:S(2)}, u32[]{:S(2)}) collective-permute-start(f32[256,256]{1,0:T(8,128)} %pad_maximum_fusion.6), channel_id=1, source_target_pairs={{0,5},{1,6},{2,7},{3,8},{4,9},{5,10},{6,11},{7,12},{8,13},{9,14},{... | collective-permute-start | bytes 786440 | tf_op jit(solution)/shard_map/ppermute | solution.py:159
  78.5 2.7 %copy-start = (f32[256,256]{1,0:T(8,128)}, f32[256,256]{1,0:T(8,128)S(1)}, u32[]{:S(2)}) copy-start(f32[256,256]{1,0:T(8,128)S(1)} %collective-permute-done.8) | copy-start | bytes 786436
  78.5 21.9 %collective-permute-start.18 = (f32[256,256]{1,0:T(8,128)S(1)}, f32[256,256]{1,0:T(8,128)}, u32[]{:S(2)}, u32[]{:S(2)}) collective-permute-start(f32[256,256]{1,0:T(8,128)S(1)} %concatenate.48), channel_id=1, source_target_pairs={{0,6},{1,7},{2,8},{3,9},{4,10},{5,11},{6,12},{7,13},{8,14},{9,15},... | collective-permute-start | bytes 786440 | tf_op jit(solution)/shard_map/ppermute | solution.py:159
  82.3 21.2 %collective-permute-start.11 = (f32[128,256]{1,0:T(8,128)}, f32[128,256]{1,0:T(8,128)S(1)}, u32[]{:S(2)}, u32[]{:S(2)}) collective-permute-start(f32[128,256]{1,0:T(8,128)} %get-tuple-element.10), channel_id=1, source_target_pairs={{3,0},{4,1},{5,2},{6,3},{7,4},{8,5},{9,6},{10,7},{11,8},{12,9},{13... | collective-permute-start | bytes 393224 | tf_op jit(solution)/shard_map/ppermute | solution.py:158
  87.1 16.5 %collective-permute-start.15 = (f32[128,256]{1,0:T(8,128)}, f32[128,256]{1,0:T(8,128)S(1)}, u32[]{:S(2)}, u32[]{:S(2)}) collective-permute-start(f32[128,256]{1,0:T(8,128)} %get-tuple-element.11), channel_id=1, source_target_pairs={{5,0},{6,1},{7,2},{8,3},{9,4},{10,5},{11,6},{12,7},{13,8},{14,9},{... | collective-permute-start | bytes 393224 | tf_op jit(solution)/shard_map/ppermute | solution.py:158
  91.3 12.2 %collective-permute-start.17 = (f32[128,256]{1,0:T(8,128)}, f32[128,256]{1,0:T(8,128)S(1)}, u32[]{:S(2)}, u32[]{:S(2)}) collective-permute-start(f32[128,256]{1,0:T(8,128)} %get-tuple-element.16), channel_id=1, source_target_pairs={{6,0},{7,1},{8,2},{9,3},{10,4},{11,5},{12,6},{13,7},{14,8},{15,9},... | collective-permute-start | bytes 393224 | tf_op jit(solution)/shard_map/ppermute | solution.py:158
  93.3 10.3 %collective-permute-start.9 = (f32[128,256]{1,0:T(8,128)}, f32[128,256]{1,0:T(8,128)S(1)}, u32[]{:S(2)}, u32[]{:S(2)}) collective-permute-start(f32[128,256]{1,0:T(8,128)} %get-tuple-element.13), channel_id=1, source_target_pairs={{2,0},{3,1},{4,2},{5,3},{6,4},{7,5},{8,6},{9,7},{10,8},{11,9},{12,... | collective-permute-start | bytes 393224 | tf_op jit(solution)/shard_map/ppermute | solution.py:158
  100.4 6.3 %collective-permute-start.7 = (f32[128,256]{1,0:T(8,128)S(1)}, f32[128,256]{1,0:T(8,128)S(1)}, u32[]{:S(2)}, u32[]{:S(2)}) collective-permute-start(f32[128,256]{1,0:T(8,128)S(1)} %get-tuple-element.3), channel_id=1, source_target_pairs={{1,0},{2,1},{3,2},{4,3},{5,4},{6,5},{7,6},{8,7},{9,8},{10,9},{11,1... | collective-permute-start | bytes 393224 | tf_op jit(solution)/shard_map/ppermute | solution.py:158

commit v2 on v1

--- a/solution.py
+++ b/solution.py
@@ -48,14 +48,25 @@
     chip = jnp.stack([even_part[0], odd_part[0], even_part[1], odd_part[1]])
     lows = {0: chip[0], 1: chip[1]}
     highs = {0: chip[2], 1: chip[3]}
+    fold_lows = set()
+    for r in range(REACH):
+        for j in range(r + 1, REACH + 1):
+            kind, at = fold_source(r, j)
+            fold_lows.add((count - 1 - r) % 2 + {"above": at, "own": 0, "below": -at}[kind])
     for j in range(1, REACH // 2 + 1):
         up = [(s, s + 2 * j) for s in range(count - 2 * j)]
         down = [(s, s - 2 * j) for s in range(2 * j, count)]
         below_chip = lax.ppermute(chip[:2], AXES, up)
-        above_chip = lax.ppermute(chip, AXES, down)
         lows[-2 * j], lows[1 - 2 * j] = below_chip[0], below_chip[1]
-        lows[2 * j], lows[2 * j + 1] = above_chip[0], above_chip[1]
-        highs[2 * j], highs[2 * j + 1] = above_chip[2], above_chip[3]
+        if fold_lows & {2 * j, 2 * j + 1}:
+            above_chip = lax.ppermute(chip, AXES, down)
+        else:
+            above_chip = lax.ppermute(chip[2:], AXES, down)
+        if fold_lows & {2 * j, 2 * j + 1}:
+            lows[2 * j], lows[2 * j + 1] = above_chip[0], above_chip[1]
+            highs[2 * j], highs[2 * j + 1] = above_chip[2], above_chip[3]
+        else:
+            highs[2 * j], highs[2 * j + 1] = above_chip[0], above_chip[1]
 
     def by_parity(table, t):
         return jnp.where(odd, table[t + 1], table[t])
@@ -156,10 +167,17 @@
         up = [(s + k, s) for s in range(count - k)]
         down = [(s - k, s) for s in range(k, count)]
         sent_low = lax.ppermute(low_parts[REACH - k] + to_below[k - 1], AXES, up)
-        back = lax.ppermute(jnp.concatenate([to_above_low[k - 1], to_high[k - 1]], 0), AXES, down)
+        if ("above", k) in routed:
+            back = lax.ppermute(
+                jnp.concatenate([to_above_low[k - 1], to_high[k - 1]], 0), AXES, down
+            )
+        else:
+            back = lax.ppermute(to_high[k - 1], AXES, down)
         grad_low = grad_low + sent_low
-        grad_low = grad_low + back[:length]
-        grad_high = grad_high + back[length:]
+        if ("above", k) in routed:
+            grad_low = grad_low + back[:length]
+            back = back[length:]
+        grad_high = grad_high + back
 
     grad_query = (
         (grad_query * factor)

time: 110 us -> 105 us (0.955)
  the two profiles are of different devices: /device:TPU:21 before, /device:TPU:19 now
where the time goes in v2:
time: 105 us; the launch traced here: 104 us
  starting transfers between devices  58.5 us (56%)
  waiting for transfers between devices  17.5 us (17%)
  other arithmetic  13.2 us (13%)
  local copies, waits for them, and re-layouts  6.51 us (6%)
  matrix products  6.44 us (6%)
  between operations  1.88 us (2%)
    ppermute x6, starting transfers between devices, on_device(): sent_low = lax.ppermute(low_parts[REACH - k] + to_below[k - 1], AXES, up)  22.5 us
    ppermute x5, starting transfers between devices, on_device(): lax.ppermute(jnp.concatenate([to_above_low[k - 1], to_high[k - 1]], 0), A...  15.7 us
    ppermute x3, starting transfers between devices, on_device(): below_chip = lax.ppermute(chip[:2], AXES, up)  9.5 us
    ppermute x1, waiting for transfers between devices, on_device(): above_chip = lax.ppermute(chip[2:], AXES, down)  8.05 us
    ppermute x2, starting transfers between devices, on_device(): above_chip = lax.ppermute(chip, AXES, down)  6.1 us
    ppermute x6, waiting for transfers between devices, on_device(): sent_low = lax.ppermute(low_parts[REACH - k] + to_below[k - 1], AXES, up)  3.96 us
    ppermute x1, waiting for transfers between devices, on_device(): back = lax.ppermute(to_high[k - 1], AXES, down)  3.95 us
    reshape x2, local copies, waits for them, and re-layouts, in_sequence_order(): paired = rows.reshape((2, length) + rows.shape[1:])  2.63 us
  transfers between devices with their start and end apart: 19, of which 5 were waited for; matrix products, arithmetic and copies ran while one was open for 10% of the time, Pallas kernels for 0%

profile of v2, /device:TPU:19, one launch (start us, length us, event | category | flops | bytes accessed | tf_op | source)
XLA Modules:
  0.0 104.0 jit_solution(602157638366950269)
XLA Ops:
  10.3 3.2 %collective-permute-start.1 = (bf16[2,128,256]{2,1,0:T(8,128)(2,1)S(1)}, bf16[2,128,256]{2,1,0:T(8,128)(2,1)S(1)}, u32[]{:S(2)}, u32[]{:S(2)}) collective-permute-start(bf16[2,128,256]{2,1,0:T(8,128)(2,1)S(1)} %pad_maximum_fusion.10), channel_id=1, source_target_pairs={{0,6},{1,7},{2,8},{3,9},{4,10},{5,11},{6,12},{7,13},{8,14},{9,15},... | collective-permute-start | bytes 393224 | tf_op jit(solution)/shard_map/ppermute | solution.py:59
  13.6 3.1 %collective-permute-start.2 = (bf16[2,128,256]{2,1,0:T(8,128)(2,1)S(1)}, bf16[2,128,256]{2,1,0:T(8,128)(2,1)S(1)}, u32[]{:S(2)}, u32[]{:S(2)}) collective-permute-start(bf16[2,128,256]{2,1,0:T(8,128)(2,1)S(1)} %pad_maximum_fusion.10), channel_id=1, source_target_pairs={{0,4},{1,5},{2,6},{3,7},{4,8},{5,9},{6,10},{7,11},{8,12},{9,13},{1... | collective-permute-start | bytes 393224 | tf_op jit(solution)/shard_map/ppermute | solution.py:59
  16.8 3.0 %collective-permute-start.4 = (bf16[4,128,256]{2,1,0:T(8,128)(2,1)S(1)}, bf16[4,128,256]{2,1,0:T(8,128)(2,1)S(1)}, u32[]{:S(2)}, u32[]{:S(2)}) collective-permute-start(bf16[4,128,256]{2,1,0:T(8,128)(2,1)S(1)} %pad_maximum_fusion.1), channel_id=1, source_target_pairs={{4,0},{5,1},{6,2},{7,3},{8,4},{9,5},{10,6},{11,7},{12,8},{13,9},{1... | collective-permute-start | bytes 786440 | tf_op jit(solution)/shard_map/ppermute | solution.py:62
  19.8 3.1 %collective-permute-start.6 = (bf16[4,128,256]{2,1,0:T(8,128)(2,1)S(1)}, bf16[4,128,256]{2,1,0:T(8,128)(2,1)S(1)}, u32[]{:S(2)}, u32[]{:S(2)}) collective-permute-start(bf16[4,128,256]{2,1,0:T(8,128)(2,1)S(1)} %pad_maximum_fusion.1), channel_id=1, source_target_pairs={{2,0},{3,1},{4,2},{5,3},{6,4},{7,5},{8,6},{9,7},{10,8},{11,9},{12,... | collective-permute-start | bytes 786440 | tf_op jit(solution)/shard_map/ppermute | solution.py:62
  22.9 3.1 %collective-permute-start.3 = (bf16[2,128,256]{2,1,0:T(8,128)(2,1)S(1)}, bf16[2,128,256]{2,1,0:T(8,128)(2,1)S(1)}, u32[]{:S(2)}, u32[]{:S(2)}) collective-permute-start(bf16[2,128,256]{2,1,0:T(8,128)(2,1)S(1)} %pad_maximum_fusion.10), channel_id=1, source_target_pairs={{0,2},{1,3},{2,4},{3,5},{4,6},{5,7},{6,8},{7,9},{8,10},{9,11},{10,... | collective-permute-start | bytes 393224 | tf_op jit(solution)/shard_map/ppermute | solution.py:59
  26.0 2.0 %collective-permute-start.5 = (bf16[2,128,256]{2,1,0:T(8,128)(2,1)S(1)}, bf16[2,128,256]{2,1,0:T(8,128)(2,1)S(1)}, u32[]{:S(2)}, u32[]{:S(2)}) collective-permute-start(bf16[2,128,256]{2,1,0:T(8,128)(2,1)S(1)} %pad_maximum_fusion.11), channel_id=1, source_target_pairs={{6,0},{7,1},{8,2},{9,3},{10,4},{11,5},{12,6},{13,7},{14,8},{15,9},... | collective-permute-start | bytes 393224 | tf_op jit(solution)/shard_map/ppermute | solution.py:64
  28.2 8.1 %collective-permute-done.5 = bf16[2,128,256]{2,1,0:T(8,128)(2,1)S(1)} collective-permute-done((bf16[2,128,256]{2,1,0:T(8,128)(2,1)S(1)}, bf16[2,128,256]{2,1,0:T(8,128)(2,1)S(1)}, u32[]{:S(2)}, u32[]{:S(2)}) %collective-permute-start.5) | collective-permute-done | bytes 131104 | tf_op jit(solution)/shard_map/ppermute | solution.py:64
  39.3 1.5 %fusion.6 = f32[2,8,128]{2,1,0:T(8,128)S(1)} fusion(f32[2,896,128,8]{2,1,3,0:T(8,128)S(1)} %get-tuple-element.49, f32[2,8,128]{2,1,0:T(8,128)S(1)} %get-tuple-element.48, pred[2,128,896]{1,2,0:T(8,128)(4,1)S(1)} %compare_and_fusion), kind=kLoop, calls=%fused_computation.11 | loop fusion | flops 7337984 | bytes 7585792 | tf_op jit(solution)/shard_map/reduce_sum | solution.py:127
  40.9 2.0 %fusion = (f32[2,8,128]{2,1,0:T(8,128)S(1)}, f32[2,896,128,8]{2,1,3,0:T(8,128)S(1)}) fusion(f32[2,896,128,8]{2,1,3,0:T(8,128)S(1)} %get-tuple-element.49, f32[2,8,128]{2,1,0:T(8,128)S(1)} %log_add_fusion, pred[2,128,896]{1,2,0:T(8,128)(4,1)S(1)} %compare_and_fusion, bf16[2,128,8,128]{1,3,2,0:T(8,128)(2,1)S(1)} %bitcast.244, ...), kind=kOutput, calls=%fused_computation.2 | convolution fusion | flops 479852544 | bytes 16367616 | tf_op jit(solution)/shard_map/qbhd,qwd->qhbw/dot_general | solution.py:121
  44.2 2.1 %fusion.2 = bf16[2,8,128,896]{2,3,1,0:T(8,128)(2,1)S(1)} fusion(f32[2,896,128,8]{2,1,3,0:T(8,128)S(1)} %get-tuple-element.51, f32[2,896,128,8]{2,1,3,0:T(8,128)S(1)} %get-tuple-element.49, f32[2,8,128]{2,1,0:T(8,128)S(1)} %get-tuple-element.50, f32[2,8,128]{2,1,0:T(8,128)S(1)} %log_add_fusion, pred[2,128,896]{1,2,0:T(8,128)(4,1)S(1)} %compare_and_fusion), kind=kLoop, calls=%fused_computation.4 | loop fusion | flops 11010048 | bytes 18595840 | tf_op jit(solution)/shard_map/convert_element_type | solution.py:132
  48.4 2.1 %collective-permute-start.8 = (f32[256,256]{1,0:T(8,128)S(1)}, f32[256,256]{1,0:T(8,128)}, u32[]{:S(2)}, u32[]{:S(2)}) collective-permute-start(f32[256,256]{1,0:T(8,128)S(1)} %pad_maximum_fusion.2), channel_id=1, source_target_pairs={{0,1},{1,2},{2,3},{3,4},{4,5},{5,6},{6,7},{7,8},{8,9},{9,10},{10,1... | collective-permute-start | bytes 786440 | tf_op jit(solution)/shard_map/ppermute | solution.py:171
  50.6 2.3 %collective-permute-start.10 = (f32[256,256]{1,0:T(8,128)S(1)}, f32[256,256]{1,0:T(8,128)}, u32[]{:S(2)}, u32[]{:S(2)}) collective-permute-start(f32[256,256]{1,0:T(8,128)S(1)} %pad_maximum_fusion.3), channel_id=1, source_target_pairs={{0,2},{1,3},{2,4},{3,5},{4,6},{5,7},{6,8},{7,9},{8,10},{9,11},{10,... | collective-permute-start | bytes 786440 | tf_op jit(solution)/shard_map/ppermute | solution.py:171
  52.9 2.1 %collective-permute-start.12 = (f32[256,256]{1,0:T(8,128)S(1)}, f32[256,256]{1,0:T(8,128)}, u32[]{:S(2)}, u32[]{:S(2)}) collective-permute-start(f32[256,256]{1,0:T(8,128)S(1)} %pad_maximum_fusion.4), channel_id=1, source_target_pairs={{0,3},{1,4},{2,5},{3,6},{4,7},{5,8},{6,9},{7,10},{8,11},{9,12},{10... | collective-permute-start | bytes 786440 | tf_op jit(solution)/shard_map/ppermute | solution.py:171
  55.0 1.9 %collective-permute-start.18 = (f32[128,256]{1,0:T(8,128)S(1)}, f32[128,256]{1,0:T(8,128)S(1)}, u32[]{:S(2)}, u32[]{:S(2)}) collective-permute-start(f32[128,256]{1,0:T(8,128)S(1)} %get-tuple-element.3), channel_id=1, source_target_pairs={{0,6},{1,7},{2,8},{3,9},{4,10},{5,11},{6,12},{7,13},{8,14},{9,15},... | collective-permute-start | bytes 393224 | tf_op jit(solution)/shard_map/ppermute | solution.py:175
  56.9 5.9 %collective-permute-start.13 = (f32[128,256]{1,0:T(8,128)S(1)}, f32[128,256]{1,0:T(8,128)S(1)}, u32[]{:S(2)}, u32[]{:S(2)}) collective-permute-start(f32[128,256]{1,0:T(8,128)S(1)} %get-tuple-element.34), channel_id=1, source_target_pairs={{4,0},{5,1},{6,2},{7,3},{8,4},{9,5},{10,6},{11,7},{12,8},{13,9},{1... | collective-permute-start | bytes 393224 | tf_op jit(solution)/shard_map/ppermute | solution.py:169
  64.3 4.0 %collective-permute-done.18 = f32[128,256]{1,0:T(8,128)S(1)} collective-permute-done((f32[128,256]{1,0:T(8,128)S(1)}, f32[128,256]{1,0:T(8,128)S(1)}, u32[]{:S(2)}, u32[]{:S(2)}) %collective-permute-start.18) | collective-permute-done | bytes 131104 | tf_op jit(solution)/shard_map/ppermute | solution.py:175
  68.3 3.9 %collective-permute-start.14 = (f32[256,256]{1,0:T(8,128)}, f32[256,256]{1,0:T(8,128)}, u32[]{:S(2)}, u32[]{:S(2)}) collective-permute-start(f32[256,256]{1,0:T(8,128)} %pad_maximum_fusion.5), channel_id=1, source_target_pairs={{0,4},{1,5},{2,6},{3,7},{4,8},{5,9},{6,10},{7,11},{8,12},{9,13},{1... | collective-permute-start | bytes 786440 | tf_op jit(solution)/shard_map/ppermute | solution.py:171
  72.2 5.3 %collective-permute-start.16 = (f32[256,256]{1,0:T(8,128)}, f32[256,256]{1,0:T(8,128)}, u32[]{:S(2)}, u32[]{:S(2)}) collective-permute-start(f32[256,256]{1,0:T(8,128)} %pad_maximum_fusion.6), channel_id=1, source_target_pairs={{0,5},{1,6},{2,7},{3,8},{4,9},{5,10},{6,11},{7,12},{8,13},{9,14},{... | collective-permute-start | bytes 786440 | tf_op jit(solution)/shard_map/ppermute | solution.py:171
  79.5 2.7 %collective-permute-start.11 = (f32[128,256]{1,0:T(8,128)}, f32[128,256]{1,0:T(8,128)S(1)}, u32[]{:S(2)}, u32[]{:S(2)}) collective-permute-start(f32[128,256]{1,0:T(8,128)} %get-tuple-element.11), channel_id=1, source_target_pairs={{3,0},{4,1},{5,2},{6,3},{7,4},{8,5},{9,6},{10,7},{11,8},{12,9},{13... | collective-permute-start | bytes 393224 | tf_op jit(solution)/shard_map/ppermute | solution.py:169
  82.1 3.7 %collective-permute-start.15 = (f32[128,256]{1,0:T(8,128)}, f32[128,256]{1,0:T(8,128)S(1)}, u32[]{:S(2)}, u32[]{:S(2)}) collective-permute-start(f32[128,256]{1,0:T(8,128)} %get-tuple-element.12), channel_id=1, source_target_pairs={{5,0},{6,1},{7,2},{8,3},{9,4},{10,5},{11,6},{12,7},{13,8},{14,9},{... | collective-permute-start | bytes 393224 | tf_op jit(solution)/shard_map/ppermute | solution.py:169
  85.9 2.8 %collective-permute-start.17 = (f32[128,256]{1,0:T(8,128)}, f32[128,256]{1,0:T(8,128)S(1)}, u32[]{:S(2)}, u32[]{:S(2)}) collective-permute-start(f32[128,256]{1,0:T(8,128)} %get-tuple-element.17), channel_id=1, source_target_pairs={{6,0},{7,1},{8,2},{9,3},{10,4},{11,5},{12,6},{13,7},{14,8},{15,9},... | collective-permute-start | bytes 393224 | tf_op jit(solution)/shard_map/ppermute | solution.py:169
  88.7 5.5 %collective-permute-start.9 = (f32[128,256]{1,0:T(8,128)}, f32[128,256]{1,0:T(8,128)S(1)}, u32[]{:S(2)}, u32[]{:S(2)}) collective-permute-start(f32[128,256]{1,0:T(8,128)} %get-tuple-element.14), channel_id=1, source_target_pairs={{2,0},{3,1},{4,2},{5,3},{6,4},{7,5},{8,6},{9,7},{10,8},{11,9},{12,... | collective-permute-start | bytes 393224 | tf_op jit(solution)/shard_map/ppermute | solution.py:169
  94.2 1.9 %collective-permute-start.7 = (f32[128,256]{1,0:T(8,128)S(1)}, f32[128,256]{1,0:T(8,128)S(1)}, u32[]{:S(2)}, u32[]{:S(2)}) collective-permute-start(f32[128,256]{1,0:T(8,128)S(1)} %get-tuple-element.5), channel_id=1, source_target_pairs={{1,0},{2,1},{3,2},{4,3},{5,4},{6,5},{7,6},{8,7},{9,8},{10,9},{11,1... | collective-permute-start | bytes 393224 | tf_op jit(solution)/shard_map/ppermute | solution.py:169
  97.6 3.8 %collective-permute-done.7 = f32[128,256]{1,0:T(8,128)S(1)} collective-permute-done((f32[128,256]{1,0:T(8,128)S(1)}, f32[128,256]{1,0:T(8,128)S(1)}, u32[]{:S(2)}, u32[]{:S(2)}) %collective-permute-start.7) | collective-permute-done | bytes 131104 | tf_op jit(solution)/shard_map/ppermute | solution.py:169
  (76 shorter events, 23.0 us)
Async XLA Ops:
  3.5 6.7 %collective-permute-start = (bf16[2,128,256]{2,1,0:T(8,128)(2,1)S(1)}, bf16[2,128,256]{2,1,0:T(8,128)(2,1)S(1)}, u32[]{:S(2)}, u32[]{:S(2)}) collective-permute-start(bf16[2,128,256]{2,1,0:T(8,128)(2,1)S(1)} %reverse_select_fusion.3), channel_id=1, source_target_pairs={{0,1},{1,0},{2,3},{3,2},{4,5},{5,4},{6,7},{7,6},{8,9},{9,8},{10,11... | collective-permute-start | bytes 393224 | tf_op jit(solution)/shard_map/ppermute | solution.py:45
  10.3 15.7 %collective-permute-start.1 = (bf16[2,128,256]{2,1,0:T(8,128)(2,1)S(1)}, bf16[2,128,256]{2,1,0:T(8,128)(2,1)S(1)}, u32[]{:S(2)}, u32[]{:S(2)}) collective-permute-start(bf16[2,128,256]{2,1,0:T(8,128)(2,1)S(1)} %pad_maximum_fusion.10), channel_id=1, source_target_pairs={{0,6},{1,7},{2,8},{3,9},{4,10},{5,11},{6,12},{7,13},{8,14},{9,15},... | collective-permute-start | bytes 393224 | tf_op jit(solution)/shard_map/ppermute | solution.py:59
  13.6 14.6 %collective-permute-start.2 = (bf16[2,128,256]{2,1,0:T(8,128)(2,1)S(1)}, bf16[2,128,256]{2,1,0:T(8,128)(2,1)S(1)}, u32[]{:S(2)}, u32[]{:S(2)}) collective-permute-start(bf16[2,128,256]{2,1,0:T(8,128)(2,1)S(1)} %pad_maximum_fusion.10), channel_id=1, source_target_pairs={{0,4},{1,5},{2,6},{3,7},{4,8},{5,9},{6,10},{7,11},{8,12},{9,13},{1... | collective-permute-start | bytes 393224 | tf_op jit(solution)/shard_map/ppermute | solution.py:59
  16.8 19.5 %collective-permute-start.4 = (bf16[4,128,256]{2,1,0:T(8,128)(2,1)S(1)}, bf16[4,128,256]{2,1,0:T(8,128)(2,1)S(1)}, u32[]{:S(2)}, u32[]{:S(2)}) collective-permute-start(bf16[4,128,256]{2,1,0:T(8,128)(2,1)S(1)} %pad_maximum_fusion.1), channel_id=1, source_target_pairs={{4,0},{5,1},{6,2},{7,3},{8,4},{9,5},{10,6},{11,7},{12,8},{13,9},{1... | collective-permute-start | bytes 786440 | tf_op jit(solution)/shard_map/ppermute | solution.py:62
  19.8 18.0 %collective-permute-start.6 = (bf16[4,128,256]{2,1,0:T(8,128)(2,1)S(1)}, bf16[4,128,256]{2,1,0:T(8,128)(2,1)S(1)}, u32[]{:S(2)}, u32[]{:S(2)}) collective-permute-start(bf16[4,128,256]{2,1,0:T(8,128)(2,1)S(1)} %pad_maximum_fusion.1), channel_id=1, source_target_pairs={{2,0},{3,1},{4,2},{5,3},{6,4},{7,5},{8,6},{9,7},{10,8},{11,9},{12,... | collective-permute-start | bytes 786440 | tf_op jit(solution)/shard_map/ppermute | solution.py:62
  22.9 14.9 %collective-permute-start.3 = (bf16[2,128,256]{2,1,0:T(8,128)(2,1)S(1)}, bf16[2,128,256]{2,1,0:T(8,128)(2,1)S(1)}, u32[]{:S(2)}, u32[]{:S(2)}) collective-permute-start(bf16[2,128,256]{2,1,0:T(8,128)(2,1)S(1)} %pad_maximum_fusion.10), channel_id=1, source_target_pairs={{0,2},{1,3},{2,4},{3,5},{4,6},{5,7},{6,8},{7,9},{8,10},{9,11},{10,... | collective-permute-start | bytes 393224 | tf_op jit(solution)/shard_map/ppermute | solution.py:59
  26.0 10.2 %collective-permute-start.5 = (bf16[2,128,256]{2,1,0:T(8,128)(2,1)S(1)}, bf16[2,128,256]{2,1,0:T(8,128)(2,1)S(1)}, u32[]{:S(2)}, u32[]{:S(2)}) collective-permute-start(bf16[2,128,256]{2,1,0:T(8,128)(2,1)S(1)} %pad_maximum_fusion.11), channel_id=1, source_target_pairs={{6,0},{7,1},{8,2},{9,3},{10,4},{11,5},{12,6},{13,7},{14,8},{15,9},... | collective-permute-start | bytes 393224 | tf_op jit(solution)/shard_map/ppermute | solution.py:64
  48.4 31.1 %collective-permute-start.8 = (f32[256,256]{1,0:T(8,128)S(1)}, f32[256,256]{1,0:T(8,128)}, u32[]{:S(2)}, u32[]{:S(2)}) collective-permute-start(f32[256,256]{1,0:T(8,128)S(1)} %pad_maximum_fusion.2), channel_id=1, source_target_pairs={{0,1},{1,2},{2,3},{3,4},{4,5},{5,6},{6,7},{7,8},{8,9},{9,10},{10,1... | collective-permute-start | bytes 786440 | tf_op jit(solution)/shard_map/ppermute | solution.py:171
  50.6 31.5 %collective-permute-start.10 = (f32[256,256]{1,0:T(8,128)S(1)}, f32[256,256]{1,0:T(8,128)}, u32[]{:S(2)}, u32[]{:S(2)}) collective-permute-start(f32[256,256]{1,0:T(8,128)S(1)} %pad_maximum_fusion.3), channel_id=1, source_target_pairs={{0,2},{1,3},{2,4},{3,5},{4,6},{5,7},{6,8},{7,9},{8,10},{9,11},{10,... | collective-permute-start | bytes 786440 | tf_op jit(solution)/shard_map/ppermute | solution.py:171
  52.9 33.0 %collective-permute-start.12 = (f32[256,256]{1,0:T(8,128)S(1)}, f32[256,256]{1,0:T(8,128)}, u32[]{:S(2)}, u32[]{:S(2)}) collective-permute-start(f32[256,256]{1,0:T(8,128)S(1)} %pad_maximum_fusion.4), channel_id=1, source_target_pairs={{0,3},{1,4},{2,5},{3,6},{4,7},{5,8},{6,9},{7,10},{8,11},{9,12},{10... | collective-permute-start | bytes 786440 | tf_op jit(solution)/shard_map/ppermute | solution.py:171
  55.0 13.3 %collective-permute-start.18 = (f32[128,256]{1,0:T(8,128)S(1)}, f32[128,256]{1,0:T(8,128)S(1)}, u32[]{:S(2)}, u32[]{:S(2)}) collective-permute-start(f32[128,256]{1,0:T(8,128)S(1)} %get-tuple-element.3), channel_id=1, source_target_pairs={{0,6},{1,7},{2,8},{3,9},{4,10},{5,11},{6,12},{7,13},{8,14},{9,15},... | collective-permute-start | bytes 393224 | tf_op jit(solution)/shard_map/ppermute | solution.py:175
  56.9 15.2 %collective-permute-start.13 = (f32[128,256]{1,0:T(8,128)S(1)}, f32[128,256]{1,0:T(8,128)S(1)}, u32[]{:S(2)}, u32[]{:S(2)}) collective-permute-start(f32[128,256]{1,0:T(8,128)S(1)} %get-tuple-element.34), channel_id=1, source_target_pairs={{4,0},{5,1},{6,2},{7,3},{8,4},{9,5},{10,6},{11,7},{12,8},{13,9},{1... | collective-permute-start | bytes 393224 | tf_op jit(solution)/shard_map/ppermute | solution.py:169
  68.3 3.9 %copy-start.1 = (f32[128,256]{1,0:T(8,128)}, f32[128,256]{1,0:T(8,128)S(1)}, u32[]{:S(2)}) copy-start(f32[128,256]{1,0:T(8,128)S(1)} %collective-permute-done.18) | copy-start | bytes 393220
  68.3 20.3 %collective-permute-start.14 = (f32[256,256]{1,0:T(8,128)}, f32[256,256]{1,0:T(8,128)}, u32[]{:S(2)}, u32[]{:S(2)}) collective-permute-start(f32[256,256]{1,0:T(8,128)} %pad_maximum_fusion.5), channel_id=1, source_target_pairs={{0,4},{1,5},{2,6},{3,7},{4,8},{5,9},{6,10},{7,11},{8,12},{9,13},{1... | collective-permute-start | bytes 786440 | tf_op jit(solution)/shard_map/ppermute | solution.py:171
  72.2 6.2 %copy-start = (f32[128,256]{1,0:T(8,128)}, f32[128,256]{1,0:T(8,128)S(1)}, u32[]{:S(2)}) copy-start(f32[128,256]{1,0:T(8,128)S(1)} %collective-permute-done.13) | copy-start | bytes 393220
  72.2 22.0 %collective-permute-start.16 = (f32[256,256]{1,0:T(8,128)}, f32[256,256]{1,0:T(8,128)}, u32[]{:S(2)}, u32[]{:S(2)}) collective-permute-start(f32[256,256]{1,0:T(8,128)} %pad_maximum_fusion.6), channel_id=1, source_target_pairs={{0,5},{1,6},{2,7},{3,8},{4,9},{5,10},{6,11},{7,12},{8,13},{9,14},{... | collective-permute-start | bytes 786440 | tf_op jit(solution)/shard_map/ppermute | solution.py:171
  79.5 17.9 %collective-permute-start.11 = (f32[128,256]{1,0:T(8,128)}, f32[128,256]{1,0:T(8,128)S(1)}, u32[]{:S(2)}, u32[]{:S(2)}) collective-permute-start(f32[128,256]{1,0:T(8,128)} %get-tuple-element.11), channel_id=1, source_target_pairs={{3,0},{4,1},{5,2},{6,3},{7,4},{8,5},{9,6},{10,7},{11,8},{12,9},{13... | collective-permute-start | bytes 393224 | tf_op jit(solution)/shard_map/ppermute | solution.py:169
  82.1 15.3 %collective-permute-start.15 = (f32[128,256]{1,0:T(8,128)}, f32[128,256]{1,0:T(8,128)S(1)}, u32[]{:S(2)}, u32[]{:S(2)}) collective-permute-start(f32[128,256]{1,0:T(8,128)} %get-tuple-element.12), channel_id=1, source_target_pairs={{5,0},{6,1},{7,2},{8,3},{9,4},{10,5},{11,6},{12,7},{13,8},{14,9},{... | collective-permute-start | bytes 393224 | tf_op jit(solution)/shard_map/ppermute | solution.py:169
  85.9 11.5 %collective-permute-start.17 = (f32[128,256]{1,0:T(8,128)}, f32[128,256]{1,0:T(8,128)S(1)}, u32[]{:S(2)}, u32[]{:S(2)}) collective-permute-start(f32[128,256]{1,0:T(8,128)} %get-tuple-element.17), channel_id=1, source_target_pairs={{6,0},{7,1},{8,2},{9,3},{10,4},{11,5},{12,6},{13,7},{14,8},{15,9},... | collective-permute-start | bytes 393224 | tf_op jit(solution)/shard_map/ppermute | solution.py:169
  88.7 8.9 %collective-permute-start.9 = (f32[128,256]{1,0:T(8,128)}, f32[128,256]{1,0:T(8,128)S(1)}, u32[]{:S(2)}, u32[]{:S(2)}) collective-permute-start(f32[128,256]{1,0:T(8,128)} %get-tuple-element.14), channel_id=1, source_target_pairs={{2,0},{3,1},{4,2},{5,3},{6,4},{7,5},{8,6},{9,7},{10,8},{11,9},{12,... | collective-permute-start | bytes 393224 | tf_op jit(solution)/shard_map/ppermute | solution.py:169
  94.2 7.2 %collective-permute-start.7 = (f32[128,256]{1,0:T(8,128)S(1)}, f32[128,256]{1,0:T(8,128)S(1)}, u32[]{:S(2)}, u32[]{:S(2)}) collective-permute-start(f32[128,256]{1,0:T(8,128)S(1)} %get-tuple-element.5), channel_id=1, source_target_pairs={{1,0},{2,1},{3,2},{4,3},{5,4},{6,5},{7,6},{8,7},{9,8},{10,9},{11,1... | collective-permute-start | bytes 393224 | tf_op jit(solution)/shard_map/ppermute | solution.py:169

commit v3 on v2

--- a/solution.py
+++ b/solution.py
@@ -40,9 +40,12 @@
         paired = rows.reshape((2, length) + rows.shape[1:])
         return jnp.where(swapped, paired[::-1], paired)
 
-    own = in_sequence_order(jnp.concatenate([key_states, value_states], 1))
+    stored = jnp.concatenate([key_states, value_states], 1).reshape(2, length, 2 * head_size)
+    stored_mate = lax.ppermute(stored, AXES, [(s, s ^ 1) for s in range(count)])
+    own = jnp.where(swapped, stored[::-1], stored)
     odd = (device % 2) == 1
-    mate = lax.ppermute(own, AXES, [(s, s ^ 1) for s in range(count)])
+    mate_swapped = block_order[2 * (device ^ 1)] >= count
+    mate = jnp.where(mate_swapped, stored_mate[::-1], stored_mate)
     even_part = jnp.where(odd, mate, own)
     odd_part = jnp.where(odd, own, mate)
     chip = jnp.stack([even_part[0], odd_part[0], even_part[1], odd_part[1]])
@@ -163,6 +166,7 @@
 
     grad_low = low_parts[REACH] + to_own_low
     grad_high = high_parts[REACH]
+    received_low = []
     for k in range(1, REACH + 1):
         up = [(s + k, s) for s in range(count - k)]
         down = [(s - k, s) for s in range(k, count)]
@@ -173,11 +177,14 @@
             )
         else:
             back = lax.ppermute(to_high[k - 1], AXES, down)
-        grad_low = grad_low + sent_low
+        received_low.append(sent_low)
         if ("above", k) in routed:
             grad_low = grad_low + back[:length]
             back = back[length:]
         grad_high = grad_high + back
+    grad_low, grad_high = lax.optimization_barrier((grad_low, grad_high))
+    for sent_low in received_low:
+        grad_low = grad_low + sent_low
 
     grad_query = (
         (grad_query * factor)

time: 105 us -> 105 us (level)
  the two profiles are of different devices: /device:TPU:19 before, /device:TPU:20 now
where the time goes in v3:
time: 105 us; the launch traced here: 104 us
  starting transfers between devices  60 us (57%)
  waiting for transfers between devices  14.8 us (14%)
  other arithmetic  13.8 us (13%)
  local copies, waits for them, and re-layouts  6.59 us (6%)
  matrix products  6.43 us (6%)
  between operations  2.56 us (2%)
    ppermute x6, starting transfers between devices, on_device(): sent_low = lax.ppermute(low_parts[REACH - k] + to_below[k - 1], AXES, up)  26.6 us
    ppermute x5, starting transfers between devices, on_device(): lax.ppermute(jnp.concatenate([to_above_low[k - 1], to_high[k - 1]], 0), A...  11.3 us
    ppermute x3, starting transfers between devices, on_device(): below_chip = lax.ppermute(chip[:2], AXES, up)  10.3 us
    ppermute x6, waiting for transfers between devices, on_device(): sent_low = lax.ppermute(low_parts[REACH - k] + to_below[k - 1], AXES, up)  6.71 us
    ppermute x2, starting transfers between devices, on_device(): above_chip = lax.ppermute(chip, AXES, down)  5.76 us
    ppermute x1, waiting for transfers between devices, on_device(): above_chip = lax.ppermute(chip[2:], AXES, down)  4.46 us
    ppermute x1, starting transfers between devices, on_device(): above_chip = lax.ppermute(chip[2:], AXES, down)  4.13 us
    reshape x2, local copies, waits for them, and re-layouts, in_sequence_order(): paired = rows.reshape((2, length) + rows.shape[1:])  2.63 us
  transfers between devices with their start and end apart: 19, of which 5 were waited for; matrix products, arithmetic and copies ran while one was open for 13% of the time, Pallas kernels for 0%

profile of v3, /device:TPU:20, one launch (start us, length us, event | category | flops | bytes accessed | tf_op | source)
XLA Modules:
  0.0 104.2 jit_solution(10074939048148888531)
XLA Ops:
  10.4 4.4 %collective-permute-start.1 = (bf16[2,128,256]{2,1,0:T(8,128)(2,1)S(1)}, bf16[2,128,256]{2,1,0:T(8,128)(2,1)S(1)}, u32[]{:S(2)}, u32[]{:S(2)}) collective-permute-start(bf16[2,128,256]{2,1,0:T(8,128)(2,1)S(1)} %pad_maximum_fusion.10), channel_id=1, source_target_pairs={{0,6},{1,7},{2,8},{3,9},{4,10},{5,11},{6,12},{7,13},{8,14},{9,15},... | collective-permute-start | bytes 393224 | tf_op jit(solution)/shard_map/ppermute | solution.py:62
  14.8 3.4 %collective-permute-start.2 = (bf16[2,128,256]{2,1,0:T(8,128)(2,1)S(1)}, bf16[2,128,256]{2,1,0:T(8,128)(2,1)S(1)}, u32[]{:S(2)}, u32[]{:S(2)}) collective-permute-start(bf16[2,128,256]{2,1,0:T(8,128)(2,1)S(1)} %pad_maximum_fusion.10), channel_id=1, source_target_pairs={{0,4},{1,5},{2,6},{3,7},{4,8},{5,9},{6,10},{7,11},{8,12},{9,13},{1... | collective-permute-start | bytes 393224 | tf_op jit(solution)/shard_map/ppermute | solution.py:62
  18.3 2.4 %collective-permute-start.4 = (bf16[4,128,256]{2,1,0:T(8,128)(2,1)S(1)}, bf16[4,128,256]{2,1,0:T(8,128)(2,1)S(1)}, u32[]{:S(2)}, u32[]{:S(2)}) collective-permute-start(bf16[4,128,256]{2,1,0:T(8,128)(2,1)S(1)} %pad_maximum_fusion.1), channel_id=1, source_target_pairs={{4,0},{5,1},{6,2},{7,3},{8,4},{9,5},{10,6},{11,7},{12,8},{13,9},{1... | collective-permute-start | bytes 786440 | tf_op jit(solution)/shard_map/ppermute | solution.py:65
  20.7 3.3 %collective-permute-start.6 = (bf16[4,128,256]{2,1,0:T(8,128)(2,1)S(1)}, bf16[4,128,256]{2,1,0:T(8,128)(2,1)S(1)}, u32[]{:S(2)}, u32[]{:S(2)}) collective-permute-start(bf16[4,128,256]{2,1,0:T(8,128)(2,1)S(1)} %pad_maximum_fusion.1), channel_id=1, source_target_pairs={{2,0},{3,1},{4,2},{5,3},{6,4},{7,5},{8,6},{9,7},{10,8},{11,9},{12,... | collective-permute-start | bytes 786440 | tf_op jit(solution)/shard_map/ppermute | solution.py:65
  24.1 2.5 %collective-permute-start.3 = (bf16[2,128,256]{2,1,0:T(8,128)(2,1)S(1)}, bf16[2,128,256]{2,1,0:T(8,128)(2,1)S(1)}, u32[]{:S(2)}, u32[]{:S(2)}) collective-permute-start(bf16[2,128,256]{2,1,0:T(8,128)(2,1)S(1)} %pad_maximum_fusion.10), channel_id=1, source_target_pairs={{0,2},{1,3},{2,4},{3,5},{4,6},{5,7},{6,8},{7,9},{8,10},{9,11},{10,... | collective-permute-start | bytes 393224 | tf_op jit(solution)/shard_map/ppermute | solution.py:62
  26.6 4.1 %collective-permute-start.5 = (bf16[2,128,256]{2,1,0:T(8,128)(2,1)S(1)}, bf16[2,128,256]{2,1,0:T(8,128)(2,1)S(1)}, u32[]{:S(2)}, u32[]{:S(2)}) collective-permute-start(bf16[2,128,256]{2,1,0:T(8,128)(2,1)S(1)} %pad_maximum_fusion.11), channel_id=1, source_target_pairs={{6,0},{7,1},{8,2},{9,3},{10,4},{11,5},{12,6},{13,7},{14,8},{15,9},... | collective-permute-start | bytes 393224 | tf_op jit(solution)/shard_map/ppermute | solution.py:67
  30.8 4.5 %collective-permute-done.5 = bf16[2,128,256]{2,1,0:T(8,128)(2,1)S(1)} collective-permute-done((bf16[2,128,256]{2,1,0:T(8,128)(2,1)S(1)}, bf16[2,128,256]{2,1,0:T(8,128)(2,1)S(1)}, u32[]{:S(2)}, u32[]{:S(2)}) %collective-permute-start.5) | collective-permute-done | bytes 131104 | tf_op jit(solution)/shard_map/ppermute | solution.py:67
  40.0 2.0 %fusion = (f32[2,8,128]{2,1,0:T(8,128)S(1)}, f32[2,896,128,8]{2,1,3,0:T(8,128)S(1)}) fusion(f32[2,896,128,8]{2,1,3,0:T(8,128)S(1)} %get-tuple-element.54, f32[2,8,128]{2,1,0:T(8,128)S(1)} %log_add_fusion, pred[2,128,896]{1,2,0:T(8,128)(4,1)S(1)} %compare_and_fusion, bf16[2,128,8,128]{1,3,2,0:T(8,128)(2,1)S(1)} %bitcast.252, ...), kind=kOutput, calls=%fused_computation.2 | convolution fusion | flops 479852544 | bytes 16367616 | tf_op jit(solution)/shard_map/qbhd,qwd->qhbw/dot_general | solution.py:124
  43.3 2.1 %fusion.2 = bf16[2,8,128,896]{2,3,1,0:T(8,128)(2,1)S(1)} fusion(f32[2,896,128,8]{2,1,3,0:T(8,128)S(1)} %get-tuple-element.56, f32[2,896,128,8]{2,1,3,0:T(8,128)S(1)} %get-tuple-element.54, f32[2,8,128]{2,1,0:T(8,128)S(1)} %get-tuple-element.55, f32[2,8,128]{2,1,0:T(8,128)S(1)} %log_add_fusion, pred[2,128,896]{1,2,0:T(8,128)(4,1)S(1)} %compare_and_fusion), kind=kLoop, calls=%fused_computation.4 | loop fusion | flops 11010048 | bytes 18595840 | tf_op jit(solution)/shard_map/convert_element_type | solution.py:135
  48.1 1.9 %collective-permute-start.7 = (f32[256,256]{1,0:T(8,128)S(1)}, f32[256,256]{1,0:T(8,128)}, u32[]{:S(2)}, u32[]{:S(2)}) collective-permute-start(f32[256,256]{1,0:T(8,128)S(1)} %pad_maximum_fusion.2), channel_id=1, source_target_pairs={{0,1},{1,2},{2,3},{3,4},{4,5},{5,6},{6,7},{7,8},{8,9},{9,10},{10,1... | collective-permute-start | bytes 786440 | tf_op jit(solution)/shard_map/ppermute | solution.py:175
  50.1 2.6 %collective-permute-start.8 = (f32[256,256]{1,0:T(8,128)S(1)}, f32[256,256]{1,0:T(8,128)}, u32[]{:S(2)}, u32[]{:S(2)}) collective-permute-start(f32[256,256]{1,0:T(8,128)S(1)} %pad_maximum_fusion.3), channel_id=1, source_target_pairs={{0,2},{1,3},{2,4},{3,5},{4,6},{5,7},{6,8},{7,9},{8,10},{9,11},{10,... | collective-permute-start | bytes 786440 | tf_op jit(solution)/shard_map/ppermute | solution.py:175
  52.7 3.0 %collective-permute-start.9 = (f32[256,256]{1,0:T(8,128)S(1)}, f32[256,256]{1,0:T(8,128)}, u32[]{:S(2)}, u32[]{:S(2)}) collective-permute-start(f32[256,256]{1,0:T(8,128)S(1)} %pad_maximum_fusion.4), channel_id=1, source_target_pairs={{0,3},{1,4},{2,5},{3,6},{4,7},{5,8},{6,9},{7,10},{8,11},{9,12},{10... | collective-permute-start | bytes 786440 | tf_op jit(solution)/shard_map/ppermute | solution.py:175
  56.5 1.9 %collective-permute-start.10 = (f32[256,256]{1,0:T(8,128)}, f32[256,256]{1,0:T(8,128)}, u32[]{:S(2)}, u32[]{:S(2)}) collective-permute-start(f32[256,256]{1,0:T(8,128)} %pad_maximum_fusion.5), channel_id=1, source_target_pairs={{0,4},{1,5},{2,6},{3,7},{4,8},{5,9},{6,10},{7,11},{8,12},{9,13},{1... | collective-permute-start | bytes 786440 | tf_op jit(solution)/shard_map/ppermute | solution.py:175
  59.1 1.9 %collective-permute-start.11 = (f32[256,256]{1,0:T(8,128)}, f32[256,256]{1,0:T(8,128)}, u32[]{:S(2)}, u32[]{:S(2)}) collective-permute-start(f32[256,256]{1,0:T(8,128)} %pad_maximum_fusion.6), channel_id=1, source_target_pairs={{0,5},{1,6},{2,7},{3,8},{4,9},{5,10},{6,11},{7,12},{8,13},{9,14},{... | collective-permute-start | bytes 786440 | tf_op jit(solution)/shard_map/ppermute | solution.py:175
  63.0 1.9 %collective-permute-start.12 = (f32[128,256]{1,0:T(8,128)}, f32[128,256]{1,0:T(8,128)S(1)}, u32[]{:S(2)}, u32[]{:S(2)}) collective-permute-start(f32[128,256]{1,0:T(8,128)} %get-tuple-element.34), channel_id=1, source_target_pairs={{0,6},{1,7},{2,8},{3,9},{4,10},{5,11},{6,12},{7,13},{8,14},{9,15},... | collective-permute-start | bytes 393224 | tf_op jit(solution)/shard_map/ppermute | solution.py:179
  64.9 6.5 %collective-permute-start.15 = (f32[128,256]{1,0:T(8,128)}, f32[128,256]{1,0:T(8,128)S(1)}, u32[]{:S(2)}, u32[]{:S(2)}) collective-permute-start(f32[128,256]{1,0:T(8,128)} %get-tuple-element.16), channel_id=1, source_target_pairs={{3,0},{4,1},{5,2},{6,3},{7,4},{8,5},{9,6},{10,7},{11,8},{12,9},{13... | collective-permute-start | bytes 393224 | tf_op jit(solution)/shard_map/ppermute | solution.py:173
  71.4 3.4 %collective-permute-start.17 = (f32[128,256]{1,0:T(8,128)}, f32[128,256]{1,0:T(8,128)S(1)}, u32[]{:S(2)}, u32[]{:S(2)}) collective-permute-start(f32[128,256]{1,0:T(8,128)} %get-tuple-element.17), channel_id=1, source_target_pairs={{5,0},{6,1},{7,2},{8,3},{9,4},{10,5},{11,6},{12,7},{13,8},{14,9},{... | collective-permute-start | bytes 393224 | tf_op jit(solution)/shard_map/ppermute | solution.py:173
  74.8 10.5 %collective-permute-start.13 = (f32[128,256]{1,0:T(8,128)}, f32[128,256]{1,0:T(8,128)S(1)}, u32[]{:S(2)}, u32[]{:S(2)}) collective-permute-start(f32[128,256]{1,0:T(8,128)} %get-tuple-element.19), channel_id=1, source_target_pairs={{1,0},{2,1},{3,2},{4,3},{5,4},{6,5},{7,6},{8,7},{9,8},{10,9},{11,1... | collective-permute-start | bytes 393224 | tf_op jit(solution)/shard_map/ppermute | solution.py:173
  85.3 2.1 %collective-permute-done.11 = f32[256,256]{1,0:T(8,128)} collective-permute-done((f32[256,256]{1,0:T(8,128)}, f32[256,256]{1,0:T(8,128)}, u32[]{:S(2)}, u32[]{:S(2)}) %collective-permute-start.11) | collective-permute-done | bytes 262176 | tf_op jit(solution)/shard_map/ppermute | solution.py:175
  87.4 1.9 %collective-permute-start.14 = (f32[128,256]{1,0:T(8,128)}, f32[128,256]{1,0:T(8,128)S(1)}, u32[]{:S(2)}, u32[]{:S(2)}) collective-permute-start(f32[128,256]{1,0:T(8,128)} %get-tuple-element.14), channel_id=1, source_target_pairs={{2,0},{3,1},{4,2},{5,3},{6,4},{7,5},{8,6},{9,7},{10,8},{11,9},{12,... | collective-permute-start | bytes 393224 | tf_op jit(solution)/shard_map/ppermute | solution.py:173
  90.6 1.9 %collective-permute-start.16 = (f32[128,256]{1,0:T(8,128)}, f32[128,256]{1,0:T(8,128)S(1)}, u32[]{:S(2)}, u32[]{:S(2)}) collective-permute-start(f32[128,256]{1,0:T(8,128)} %get-tuple-element.15), channel_id=1, source_target_pairs={{4,0},{5,1},{6,2},{7,3},{8,4},{9,5},{10,6},{11,7},{12,8},{13,9},{1... | collective-permute-start | bytes 393224 | tf_op jit(solution)/shard_map/ppermute | solution.py:173
  92.5 2.3 %collective-permute-start.18 = (f32[128,256]{1,0:T(8,128)S(1)}, f32[128,256]{1,0:T(8,128)S(1)}, u32[]{:S(2)}, u32[]{:S(2)}) collective-permute-start(f32[128,256]{1,0:T(8,128)S(1)} %get-tuple-element.23), channel_id=1, source_target_pairs={{6,0},{7,1},{8,2},{9,3},{10,4},{11,5},{12,6},{13,7},{14,8},{15,9},... | collective-permute-start | bytes 393224 | tf_op jit(solution)/shard_map/ppermute | solution.py:173
  96.1 3.7 %collective-permute-done.16 = f32[128,256]{1,0:T(8,128)S(1)} collective-permute-done((f32[128,256]{1,0:T(8,128)}, f32[128,256]{1,0:T(8,128)S(1)}, u32[]{:S(2)}, u32[]{:S(2)}) %collective-permute-start.16) | collective-permute-done | bytes 131104 | tf_op jit(solution)/shard_map/ppermute | solution.py:173
  99.8 3.0 %collective-permute-done.18 = f32[128,256]{1,0:T(8,128)S(1)} collective-permute-done((f32[128,256]{1,0:T(8,128)S(1)}, f32[128,256]{1,0:T(8,128)S(1)}, u32[]{:S(2)}, u32[]{:S(2)}) %collective-permute-start.18) | collective-permute-done | bytes 131104 | tf_op jit(solution)/shard_map/ppermute | solution.py:173
  (73 shorter events, 24.4 us)
Async XLA Ops:
  1.5 8.8 %collective-permute-start = (bf16[2,128,256]{2,1,0:T(8,128)(2,1)S(1)}, bf16[2,128,256]{2,1,0:T(8,128)(2,1)S(1)}, u32[]{:S(2)}, u32[]{:S(2)}) collective-permute-start(bf16[2,128,256]{2,1,0:T(8,128)(2,1)S(1)} %bitcast.257), channel_id=1, source_target_pairs={{0,1},{1,0},{2,3},{3,2},{4,5},{5,4},{6,7},{7,6},{8,9},{9,8},{10,11... | collective-permute-start | bytes 393224 | tf_op jit(solution)/shard_map/ppermute | solution.py:44
  10.4 16.2 %collective-permute-start.1 = (bf16[2,128,256]{2,1,0:T(8,128)(2,1)S(1)}, bf16[2,128,256]{2,1,0:T(8,128)(2,1)S(1)}, u32[]{:S(2)}, u32[]{:S(2)}) collective-permute-start(bf16[2,128,256]{2,1,0:T(8,128)(2,1)S(1)} %pad_maximum_fusion.10), channel_id=1, source_target_pairs={{0,6},{1,7},{2,8},{3,9},{4,10},{5,11},{6,12},{7,13},{8,14},{9,15},... | collective-permute-start | bytes 393224 | tf_op jit(solution)/shard_map/ppermute | solution.py:62
  14.8 16.0 %collective-permute-start.2 = (bf16[2,128,256]{2,1,0:T(8,128)(2,1)S(1)}, bf16[2,128,256]{2,1,0:T(8,128)(2,1)S(1)}, u32[]{:S(2)}, u32[]{:S(2)}) collective-permute-start(bf16[2,128,256]{2,1,0:T(8,128)(2,1)S(1)} %pad_maximum_fusion.10), channel_id=1, source_target_pairs={{0,4},{1,5},{2,6},{3,7},{4,8},{5,9},{6,10},{7,11},{8,12},{9,13},{1... | collective-permute-start | bytes 393224 | tf_op jit(solution)/shard_map/ppermute | solution.py:62
  18.3 17.0 %collective-permute-start.4 = (bf16[4,128,256]{2,1,0:T(8,128)(2,1)S(1)}, bf16[4,128,256]{2,1,0:T(8,128)(2,1)S(1)}, u32[]{:S(2)}, u32[]{:S(2)}) collective-permute-start(bf16[4,128,256]{2,1,0:T(8,128)(2,1)S(1)} %pad_maximum_fusion.1), channel_id=1, source_target_pairs={{4,0},{5,1},{6,2},{7,3},{8,4},{9,5},{10,6},{11,7},{12,8},{13,9},{1... | collective-permute-start | bytes 786440 | tf_op jit(solution)/shard_map/ppermute | solution.py:65
  20.7 16.2 %collective-permute-start.6 = (bf16[4,128,256]{2,1,0:T(8,128)(2,1)S(1)}, bf16[4,128,256]{2,1,0:T(8,128)(2,1)S(1)}, u32[]{:S(2)}, u32[]{:S(2)}) collective-permute-start(bf16[4,128,256]{2,1,0:T(8,128)(2,1)S(1)} %pad_maximum_fusion.1), channel_id=1, source_target_pairs={{2,0},{3,1},{4,2},{5,3},{6,4},{7,5},{8,6},{9,7},{10,8},{11,9},{12,... | collective-permute-start | bytes 786440 | tf_op jit(solution)/shard_map/ppermute | solution.py:65
  24.1 12.8 %collective-permute-start.3 = (bf16[2,128,256]{2,1,0:T(8,128)(2,1)S(1)}, bf16[2,128,256]{2,1,0:T(8,128)(2,1)S(1)}, u32[]{:S(2)}, u32[]{:S(2)}) collective-permute-start(bf16[2,128,256]{2,1,0:T(8,128)(2,1)S(1)} %pad_maximum_fusion.10), channel_id=1, source_target_pairs={{0,2},{1,3},{2,4},{3,5},{4,6},{5,7},{6,8},{7,9},{8,10},{9,11},{10,... | collective-permute-start | bytes 393224 | tf_op jit(solution)/shard_map/ppermute | solution.py:62
  26.6 8.7 %collective-permute-start.5 = (bf16[2,128,256]{2,1,0:T(8,128)(2,1)S(1)}, bf16[2,128,256]{2,1,0:T(8,128)(2,1)S(1)}, u32[]{:S(2)}, u32[]{:S(2)}) collective-permute-start(bf16[2,128,256]{2,1,0:T(8,128)(2,1)S(1)} %pad_maximum_fusion.11), channel_id=1, source_target_pairs={{6,0},{7,1},{8,2},{9,3},{10,4},{11,5},{12,6},{13,7},{14,8},{15,9},... | collective-permute-start | bytes 393224 | tf_op jit(solution)/shard_map/ppermute | solution.py:67
  48.1 14.8 %collective-permute-start.7 = (f32[256,256]{1,0:T(8,128)S(1)}, f32[256,256]{1,0:T(8,128)}, u32[]{:S(2)}, u32[]{:S(2)}) collective-permute-start(f32[256,256]{1,0:T(8,128)S(1)} %pad_maximum_fusion.2), channel_id=1, source_target_pairs={{0,1},{1,2},{2,3},{3,4},{4,5},{5,6},{6,7},{7,8},{8,9},{9,10},{10,1... | collective-permute-start | bytes 786440 | tf_op jit(solution)/shard_map/ppermute | solution.py:175
  50.1 14.8 %collective-permute-start.8 = (f32[256,256]{1,0:T(8,128)S(1)}, f32[256,256]{1,0:T(8,128)}, u32[]{:S(2)}, u32[]{:S(2)}) collective-permute-start(f32[256,256]{1,0:T(8,128)S(1)} %pad_maximum_fusion.3), channel_id=1, source_target_pairs={{0,2},{1,3},{2,4},{3,5},{4,6},{5,7},{6,8},{7,9},{8,10},{9,11},{10,... | collective-permute-start | bytes 786440 | tf_op jit(solution)/shard_map/ppermute | solution.py:175
  52.7 18.7 %collective-permute-start.9 = (f32[256,256]{1,0:T(8,128)S(1)}, f32[256,256]{1,0:T(8,128)}, u32[]{:S(2)}, u32[]{:S(2)}) collective-permute-start(f32[256,256]{1,0:T(8,128)S(1)} %pad_maximum_fusion.4), channel_id=1, source_target_pairs={{0,3},{1,4},{2,5},{3,6},{4,7},{5,8},{6,9},{7,10},{8,11},{9,12},{10... | collective-permute-start | bytes 786440 | tf_op jit(solution)/shard_map/ppermute | solution.py:175
  56.5 18.3 %collective-permute-start.10 = (f32[256,256]{1,0:T(8,128)}, f32[256,256]{1,0:T(8,128)}, u32[]{:S(2)}, u32[]{:S(2)}) collective-permute-start(f32[256,256]{1,0:T(8,128)} %pad_maximum_fusion.5), channel_id=1, source_target_pairs={{0,4},{1,5},{2,6},{3,7},{4,8},{5,9},{6,10},{7,11},{8,12},{9,13},{1... | collective-permute-start | bytes 786440 | tf_op jit(solution)/shard_map/ppermute | solution.py:175
  59.1 28.3 %collective-permute-start.11 = (f32[256,256]{1,0:T(8,128)}, f32[256,256]{1,0:T(8,128)}, u32[]{:S(2)}, u32[]{:S(2)}) collective-permute-start(f32[256,256]{1,0:T(8,128)} %pad_maximum_fusion.6), channel_id=1, source_target_pairs={{0,5},{1,6},{2,7},{3,8},{4,9},{5,10},{6,11},{7,12},{8,13},{9,14},{... | collective-permute-start | bytes 786440 | tf_op jit(solution)/shard_map/ppermute | solution.py:175
  63.0 27.6 %collective-permute-start.12 = (f32[128,256]{1,0:T(8,128)}, f32[128,256]{1,0:T(8,128)S(1)}, u32[]{:S(2)}, u32[]{:S(2)}) collective-permute-start(f32[128,256]{1,0:T(8,128)} %get-tuple-element.34), channel_id=1, source_target_pairs={{0,6},{1,7},{2,8},{3,9},{4,10},{5,11},{6,12},{7,13},{8,14},{9,15},... | collective-permute-start | bytes 393224 | tf_op jit(solution)/shard_map/ppermute | solution.py:179
  64.9 27.6 %collective-permute-start.15 = (f32[128,256]{1,0:T(8,128)}, f32[128,256]{1,0:T(8,128)S(1)}, u32[]{:S(2)}, u32[]{:S(2)}) collective-permute-start(f32[128,256]{1,0:T(8,128)} %get-tuple-element.16), channel_id=1, source_target_pairs={{3,0},{4,1},{5,2},{6,3},{7,4},{8,5},{9,6},{10,7},{11,8},{12,9},{13... | collective-permute-start | bytes 393224 | tf_op jit(solution)/shard_map/ppermute | solution.py:173
  71.4 24.7 %collective-permute-start.17 = (f32[128,256]{1,0:T(8,128)}, f32[128,256]{1,0:T(8,128)S(1)}, u32[]{:S(2)}, u32[]{:S(2)}) collective-permute-start(f32[128,256]{1,0:T(8,128)} %get-tuple-element.17), channel_id=1, source_target_pairs={{5,0},{6,1},{7,2},{8,3},{9,4},{10,5},{11,6},{12,7},{13,8},{14,9},{... | collective-permute-start | bytes 393224 | tf_op jit(solution)/shard_map/ppermute | solution.py:173
  74.8 21.3 %collective-permute-start.13 = (f32[128,256]{1,0:T(8,128)}, f32[128,256]{1,0:T(8,128)S(1)}, u32[]{:S(2)}, u32[]{:S(2)}) collective-permute-start(f32[128,256]{1,0:T(8,128)} %get-tuple-element.19), channel_id=1, source_target_pairs={{1,0},{2,1},{3,2},{4,3},{5,4},{6,5},{7,6},{8,7},{9,8},{10,9},{11,1... | collective-permute-start | bytes 393224 | tf_op jit(solution)/shard_map/ppermute | solution.py:173
  87.4 8.7 %collective-permute-start.14 = (f32[128,256]{1,0:T(8,128)}, f32[128,256]{1,0:T(8,128)S(1)}, u32[]{:S(2)}, u32[]{:S(2)}) collective-permute-start(f32[128,256]{1,0:T(8,128)} %get-tuple-element.14), channel_id=1, source_target_pairs={{2,0},{3,1},{4,2},{5,3},{6,4},{7,5},{8,6},{9,7},{10,8},{11,9},{12,... | collective-permute-start | bytes 393224 | tf_op jit(solution)/shard_map/ppermute | solution.py:173
  90.6 9.2 %collective-permute-start.16 = (f32[128,256]{1,0:T(8,128)}, f32[128,256]{1,0:T(8,128)S(1)}, u32[]{:S(2)}, u32[]{:S(2)}) collective-permute-start(f32[128,256]{1,0:T(8,128)} %get-tuple-element.15), channel_id=1, source_target_pairs={{4,0},{5,1},{6,2},{7,3},{8,4},{9,5},{10,6},{11,7},{12,8},{13,9},{1... | collective-permute-start | bytes 393224 | tf_op jit(solution)/shard_map/ppermute | solution.py:173
  92.5 10.3 %collective-permute-start.18 = (f32[128,256]{1,0:T(8,128)S(1)}, f32[128,256]{1,0:T(8,128)S(1)}, u32[]{:S(2)}, u32[]{:S(2)}) collective-permute-start(f32[128,256]{1,0:T(8,128)S(1)} %get-tuple-element.23), channel_id=1, source_target_pairs={{6,0},{7,1},{8,2},{9,3},{10,4},{11,5},{12,6},{13,7},{14,8},{15,9},... | collective-permute-start | bytes 393224 | tf_op jit(solution)/shard_map/ppermute | solution.py:173
